TPU v7x, 32 devices: a whole 2x2x4 slice. The times are simulated.
32 devices in a mesh: grp: 2 (over x), row: 4 (over y, core), col: 4 (over z).
Axes of the slice: x: 2, y: 2, z: 4, core: 2. Of those that a mesh axis runs over, the one named last changes fastest.
Arguments:
- patches: bfloat16 [64, 64, 1024], P(('grp', 'row'), 'col'), parts along dimension 0, may hold values from -620 to 620
- upstream: bfloat16 [64, 64, 1024], P(('grp', 'row'), 'col'), parts along dimension 0, may hold values from -0.59765625 to 0.59765625
- qkv_weight: bfloat16 [1024, 3072], P('row'), may hold values from -0.1875 to 0.1875
- out_weight: bfloat16 [1024, 1024], P('row'), may hold values from -0.1875 to 0.1875
- layer_norm_gain: float32 [1024], replicated, may hold values from 0.5 to 1.5
- pos_bias: float32 [16, 49], replicated, may hold values from -3 to 300
- valid_mask: int32 [64, 64], P(('grp', 'row'), 'col'), parts along dimension 0, may hold values 0 or 1
Outputs:
- patch_gradient: float32 [64, 64, 1024], P(('grp', 'row'), 'col'), parts along dimension 0
- qkv_grad: float32 [2048, 3072], P(('grp', 'row')), parts along dimension 0
- out_grad: float32 [2048, 1024], P(('grp', 'row')), parts along dimension 0
- gain_gradient: float32 [2048], P(('grp', 'row')), parts along dimension 0
- bias_grad: float32 [32, 49], P(('grp', 'row')), parts along dimension 0
There are 2 independent parts, one for each index of `grp`. A program takes and returns all parts, laid end to end along the dimension named above; an argument that names none is the same for every part. Nothing has to cross between parts.
All inputs are finite; a program needn't handle non-finite values. No bound on the sum of `valid_mask` on one device may be relied on, other than what follows from the above.
Results may differ from a plain program's by a relative error of at most 0.012.
Values may be sent and summed in bfloat16 or wider, within the bound.
No kernel may reach another device: no remote copies, remote signals or barrier semaphores. Data moves between devices by JAX's collectives and lax.ppermute only.
A program may use at most 192 MiB of HBM per device.

v0:
```python
import jax
import jax.numpy as jnp
from jax import lax
from jax.sharding import PartitionSpec as P

RAD = 3
HIGHEST = lax.Precision.HIGHEST
HIGH = lax.Precision.HIGH


def extended_2(shard, sides, width):
    for axis, dim in sides:
        devices, length = (lax.axis_size(axis), shard.shape[dim])
        up = [(i, i + 1) for i in range(devices - 1)]
        down = [(j, i) for i, j in up]
        last = lax.slice_in_dim(shard, length - width, length, axis=dim)
        first = lax.slice_in_dim(shard, 0, width, axis=dim)
        before = lax.ppermute(last, axis, up)
        after = lax.ppermute(first, axis, down)
        shard = jnp.concatenate([before, shard, after], axis=dim)
    return shard


def passed_along(value, axis, steps):
    count = lax.axis_size(axis)
    first, last = (max(0, -steps), min(count, count - steps))
    return lax.ppermute(value, axis, [(source, source + steps) for source in range(first, last)])


def apply_layer_norm(values, norm_gain_value):
    floats = values.astype(jnp.float32)
    feature_mean = jnp.mean(floats, axis=-1, keepdims=True)
    mean_removed = floats - feature_mean
    variance = jnp.mean(mean_removed * mean_removed, axis=-1, keepdims=True)
    inverse_deviation = lax.rsqrt(variance + 1e-05)
    standardized_input = mean_removed * inverse_deviation
    return (
        (standardized_input * norm_gain_value).astype(jnp.bfloat16),
        standardized_input,
        inverse_deviation,
    )


def window_tables(rows, cols, reach):
    side = 2 * reach + 1
    shape = (rows, cols, rows + 2 * reach, cols + 2 * reach)
    row_gap = lax.broadcasted_iota(jnp.int32, shape, 2) - lax.broadcasted_iota(jnp.int32, shape, 0)
    col_gap = lax.broadcasted_iota(jnp.int32, shape, 3) - lax.broadcasted_iota(jnp.int32, shape, 1)
    inside = (row_gap >= 0) & (row_gap < side) & (col_gap >= 0) & (col_gap < side)
    offset_id = jnp.where(inside, row_gap * side + col_gap, -1)
    centre = (row_gap == reach) & (col_gap == reach)
    nq = rows * cols
    nk = (rows + 2 * reach) * (cols + 2 * reach)
    offset_id = offset_id.reshape(nq * nk)
    one_hot = (
        offset_id[None, :] == lax.broadcasted_iota(jnp.int32, (side * side, nq * nk), 0)
    ).astype(jnp.float32)
    return inside.reshape(nq, nk), centre.reshape(nq, nk), one_hot


def body(patches, upstream, qkv_weight, out_weight, layer_norm_gain, pos_bias, valid_mask):
    rows, cols, width = patches.shape
    heads = pos_bias.shape[0]
    hdim = width // heads
    reach = RAD
    ext_rows, ext_cols = rows + 2 * reach, cols + 2 * reach
    nq, nk = rows * cols, ext_rows * ext_cols
    scale = float(hdim) ** (-0.5)
    full_qkv, full_out = (
        lax.all_gather(qkv_weight, "row", axis=0, tiled=True),
        lax.all_gather(out_weight, "row", axis=0, tiled=True),
    )
    normed_features, standardized_input, inverse_deviation = apply_layer_norm(
        patches, layer_norm_gain
    )
    flat = normed_features.reshape(-1, width)
    joined = jnp.dot(flat, full_qkv, preferred_element_type=jnp.float32).astype(jnp.bfloat16)
    query = joined[:, :width]
    kv = joined[:, width:].reshape(rows, cols, 2 * width)
    kv_ext = extended_2(kv, (("row", 0), ("col", 1)), reach).reshape(nk, 2 * width)
    mask_ext = extended_2(valid_mask, (("row", 0), ("col", 1)), reach).reshape(nk)
    q3 = query.reshape(nq, heads, hdim)
    k3 = kv_ext[:, :width].reshape(nk, heads, hdim)
    v3 = kv_ext[:, width:].reshape(nk, heads, hdim)

    inside, centre, one_hot = window_tables(rows, cols, reach)
    allowed = inside & ((mask_ext[None, :] == 1) | centre)
    bias_full = jnp.dot(pos_bias, one_hot, precision=HIGHEST).reshape(heads, nq, nk)
    raw = jnp.einsum("phd,khd->hpk", q3, k3, preferred_element_type=jnp.float32)
    scores = jnp.where(allowed[None], raw * scale + bias_full, -jnp.inf)
    top = jnp.max(scores, axis=-1, keepdims=True)
    expo = jnp.exp(scores - top)
    denom = jnp.sum(expo, axis=-1, keepdims=True)
    probs = expo / denom
    attended3 = jnp.einsum(
        "hpk,khd->phd", probs, v3.astype(jnp.float32), precision=HIGH,
        preferred_element_type=jnp.float32,
    )
    attended = attended3.astype(jnp.bfloat16).reshape(nq, width)

    grad_flat = upstream.reshape(-1, width)
    out_grad = jnp.dot(attended.T, grad_flat, preferred_element_type=jnp.float32)
    out_sum = lax.psum(
        lax.psum_scatter(out_grad.astype(jnp.bfloat16), "row", scatter_dimension=0, tiled=True), "col"
    ).astype(jnp.float32)
    attended_grad = jnp.dot(grad_flat, full_out.T, preferred_element_type=jnp.float32).astype(
        jnp.bfloat16
    )
    ag3 = attended_grad.reshape(nq, heads, hdim)
    delta = jnp.sum(
        ag3.astype(jnp.float32) * attended.reshape(nq, heads, hdim).astype(jnp.float32), axis=-1
    )
    prob_grad = jnp.einsum("phd,khd->hpk", ag3, v3, preferred_element_type=jnp.float32)
    score_grad = probs * (prob_grad - delta.T[:, :, None])
    bias_term = jnp.dot(
        score_grad.reshape(heads, nq * nk), one_hot.T, precision=HIGH,
        preferred_element_type=jnp.float32,
    )
    query_grad = jnp.einsum(
        "hpk,khd->phd", score_grad, k3.astype(jnp.float32), precision=HIGH,
        preferred_element_type=jnp.float32,
    ) * scale
    key_ext_grad = jnp.einsum(
        "hpk,phd->khd", score_grad, q3.astype(jnp.float32), precision=HIGH,
        preferred_element_type=jnp.float32,
    ) * scale
    value_ext_grad = jnp.einsum(
        "hpk,phd->khd", probs, ag3.astype(jnp.float32), precision=HIGH,
        preferred_element_type=jnp.float32,
    )
    query_term = jnp.dot(
        flat.T, query_grad.reshape(nq, width).astype(jnp.bfloat16), preferred_element_type=jnp.float32
    ).astype(jnp.bfloat16)
    out_sum, query_term = lax.optimization_barrier((out_sum, query_term))
    query_sum = lax.psum(lax.psum_scatter(query_term, "row", scatter_dimension=0, tiled=True), "col")
    buffer = jnp.concatenate(
        [key_ext_grad.reshape(ext_rows, ext_cols, width), value_ext_grad.reshape(ext_rows, ext_cols, width)],
        axis=-1,
    )
    from_below = passed_along(buffer[:reach], "row", -1)
    from_above = passed_along(buffer[reach + rows :], "row", 1)
    middle = buffer[reach : reach + rows]
    middle = middle.at[:reach].add(from_above)
    middle = middle.at[rows - reach :].add(from_below)
    from_right = passed_along(middle[:, :reach].astype(jnp.bfloat16), "col", -1).astype(jnp.float32)
    from_left = passed_along(middle[:, reach + cols :].astype(jnp.bfloat16), "col", 1).astype(
        jnp.float32
    )
    inner = middle[:, reach : reach + cols]
    inner = inner.at[:, :reach].add(from_left)
    inner = inner.at[:, cols - reach :].add(from_right)
    joined_grad = jnp.concatenate(
        [query_grad.reshape(rows, cols, width), inner], axis=-1
    ).astype(jnp.bfloat16)
    joined_grad = joined_grad.reshape(-1, 3 * width)
    normed_gradient = jnp.dot(joined_grad, full_qkv.T, preferred_element_type=jnp.float32).reshape(
        rows, cols, width
    )
    gain_product = jnp.sum(normed_gradient * standardized_input, axis=(0, 1))
    scaled_features = normed_gradient * layer_norm_gain
    patch_gradient = upstream.astype(jnp.float32) + inverse_deviation * (
        scaled_features
        - jnp.mean(scaled_features, axis=-1, keepdims=True)
        - standardized_input
        * jnp.mean(scaled_features * standardized_input, axis=-1, keepdims=True)
    )
    row_count = lax.axis_size("row")
    heads_per, rows_per = heads // row_count, width // row_count
    bias_rows = jnp.pad(
        bias_term.reshape(row_count, heads_per, -1), ((0, 0), (0, rows_per - heads_per), (0, 0))
    ).reshape(width, -1)
    offsets = bias_term.shape[1]
    spare = 128 - 1 - offsets
    kv_pad = jnp.pad(joined_grad[:, width:], ((0, 0), (0, 128)))
    big = jnp.dot(flat.T, kv_pad, preferred_element_type=jnp.float32).astype(jnp.bfloat16)
    extra = jnp.concatenate(
        [gain_product[:, None], bias_rows, jnp.zeros((width, spare), jnp.float32)], axis=1
    ).astype(jnp.bfloat16)
    big = lax.dynamic_update_slice_in_dim(big, extra, 2 * width, axis=1)
    query_sum, big = lax.optimization_barrier((query_sum, big))
    big_sum = lax.psum(lax.psum_scatter(big, "row", scatter_dimension=0, tiled=True), "col")
    big_sum = big_sum.astype(jnp.float32)
    qkv_sum = jnp.concatenate([query_sum.astype(jnp.float32), big_sum[:, : 2 * width]], axis=1)
    gain_sum = big_sum[:, 2 * width]
    bias_sum = big_sum[:heads_per, 2 * width + 1 : 2 * width + 1 + offsets]
    return (patch_gradient, qkv_sum, out_sum, gain_sum, bias_sum)


def solution(mesh):
    in_specs = (
        P(("grp", "row"), "col", None),
        P(("grp", "row"), "col", None),
        P("row", None),
        P("row", None),
        P(),
        P(),
        P(("grp", "row"), "col"),
    )
    out_specs = (
        P(("grp", "row"), "col", None),
        P(("grp", "row"), None),
        P(("grp", "row"), None),
        P(("grp", "row")),
        P(("grp", "row"), None),
    )
    return jax.shard_map(body, mesh=mesh, in_specs=in_specs, out_specs=out_specs, check_vma=False)
```

profile of v0, /device:TPU:0, one launch (start us, length us, event | category | flops | bytes accessed | tf_op | source)
XLA Modules:
  0.0 381.2 jit_solution(1226005369986527152)
XLA Ops:
  8.8 2.3 collective-permute-start.4
  11.1 1.3 collective-permute-start.5
  14.9 3.1 convolution_bitcast_fusion
  18.3 4.3 %collective-permute-start.6 = (s32[14,3]{1,0:T(8,128)S(1)}, s32[14,3]{1,0:T(8,128)S(1)}, u32[]{:S(2)}, u32[]{:S(2)}) collective-permute-start(s32[14,3]{1,0:T(8,128)S(1)} %get-tuple-element.74), channel_id=1, source_target_pairs={{0,1},{1,2},{2,3},{4,5},{5,6},{6,7},{8,9},{9,10},{10,11},{12,13},{... | collective-permute-start | bytes 512 | tf_op jit(solution)/shard_map/ppermute | solution.py:18
  22.6 1.3 collective-permute-start.7
  23.9 4.5 %reshape.402 = f32[16,128,308]{2,1,0:T(8,128)} reshape(f32[16,39424]{1,0:T(8,128)S(1)} %convolution_bitcast_fusion) | data formatting | bytes 5046272 | tf_op jit(solution)/shard_map/reshape | solution.py:88
  28.4 3.5 copy.24
  32.1 26.6 %all-gather.3.cloned.1.call-done = bf16[1024,3072]{1,0:T(8,128)(2,1)} async-done(((bf16[256,3072]{1,0:T(8,128)(2,1)}), bf16[1024,3072]{1,0:T(8,128)(2,1)}) %all-gather.3.cloned.1.call-update) | async-done | bytes 6291472 | tf_op jit(solution)/shard_map/all_gather | solution.py:70
  58.7 3.8 %convolution_convert_fusion.1 = bf16[128,3072]{1,0:T(8,128)(2,1)S(1)} fusion(bf16[128,1024]{1,0:T(8,128)(2,1)S(1)} %bitcast.57, bf16[1024,3072]{1,0:T(8,128)(2,1)} %all-gather.3.cloned.1.call-done), kind=kOutput, calls=%fused_computation.9 | convolution fusion | flops 805699584 | bytes 7340032 | tf_op jit(solution)/shard_map/dot_general | solution.py:77
  62.6 1.4 collective-permute-start.1
  64.0 3.0 collective-permute-start
  69.1 3.4 collective-permute-start.2
  72.5 1.5 collective-permute-start.3
  73.9 9.0 %all-gather.5.cloned.1.call-done = bf16[1024,1024]{1,0:T(8,128)(2,1)} async-done(((bf16[256,1024]{1,0:T(8,128)(2,1)}), bf16[1024,1024]{1,0:T(8,128)(2,1)}) %all-gather.5.cloned.1.call-update) | async-done | bytes 2097168 | tf_op jit(solution)/shard_map/all_gather | solution.py:71
  82.9 2.4 convolution_convert_fusion.5
  87.1 1.6 pad_maximum_fusion.1
  88.7 1.4 reshape.399
  90.0 1.4 fusion.50
  91.4 1.2 copy.32
  92.6 1.2 copy.33
  93.8 2.9 fusion.55
  97.1 1.3 copy-done.11
  98.7 1.1 multiply_reduce_fusion
  99.8 2.0 convolution_convert_fusion.3
  101.9 3.3 convolution_bitcast_fusion.1
  105.2 2.3 copy.29
  107.5 1.8 reshape.407
  109.4 3.0 subtract_multiply_fusion
  112.4 2.1 multiply_bitcast_fusion
  114.5 3.2 copy.28
  117.7 3.0 reshape.406
  120.7 2.9 constant_dynamic-update-slice_fusion.1
  123.6 1.3 constant_dynamic-update-slice_fusion
  124.8 10.7 %reduce-scatter.4.cloned.1.call-done = bf16[256,1024]{1,0:T(8,128)(2,1)} async-done(((bf16[1024,1024]{1,0:T(8,128)(2,1)}), bf16[256,1024]{1,0:T(8,128)(2,1)}) %reduce-scatter.4.cloned.1.call-update) | async-done | bytes 524304 | tf_op jit(solution)/shard_map/reduce_scatter | solution.py:104
  135.8 1.9 fusion.9
  138.4 2.2 convolution_convert_fusion.2
  140.6 35.6 %all-reduce.6.cloned.1.call-done = bf16[256,1024]{1,0:T(8,128)(2,1)} async-done(((bf16[256,1024]{1,0:T(8,128)(2,1)}), bf16[256,1024]{1,0:T(8,128)(2,1)}) %all-reduce.6.cloned.1.call-update) | async-done | bytes 524304 | tf_op jit(solution)/shard_map/psum | solution.py:103
  176.2 2.1 convert_element_type.82
  178.4 2.4 fusion.49
  180.7 2.1 collective-permute-start.8
  182.8 1.3 collective-permute-start.9
  184.2 2.3 copy.30
  186.5 1.6 slice.207
  188.1 5.4 %dot_general.60 = f32[4,4,39424]{2,1,0:T(4,128)} reshape(f32[16,128,308]{2,1,0:T(8,128)} %copy.30) | data formatting | bytes 5046272 | tf_op jit(solution)/shard_map/dot_general | solution.py:115
  193.6 1.3 fusion.30
  194.9 1.5 fusion.29
  197.4 3.1 collective-permute-start.10
  200.5 3.4 fusion.10
  204.4 1.1 concatenate.45
  205.6 1.1 slice.212
  206.6 1.3 collective-permute-start.11
  208.0 3.6 scatter-add.16
  211.6 2.8 collective-permute-done.11
  214.4 1.1 slice_add_fusion.2
  215.5 3.0 scatter-add.19
  218.5 1.3 convert.29
  219.8 5.1 %fusion.37 = (bf16[1024]{0:T(1024)(128)(2,1)S(1)}, f32[8,16]{1,0:T(8,128)S(1)}, f32[8,16]{1,0:T(8,128)S(1)}, f32[8,16,1024]{2,1,0:T(8,128)S(1)}) fusion(bf16[8,16,1024]{2,1,0:T(8,128)(2,1)S(1)} %copy-done.5, f32[8,16]{1,0:T(8,128)S(1)} %copy-done.16, f32[8,16]{1,0:T(8,128)S(1)} %broadcast_multiply_fusion.2, f32[1024]{0:T(1024)S(1)} %copy-done.19, ...), kind=kOutput, calls=%fused_computation.57 | convolution fusion | flops 808057600 | bytes 7872512 | tf_op jit(solution)/shard_map/dot_general | solution.py:156
  225.5 3.4 convolution_convert_fusion
  229.8 34.4 %all-reduce.8.cloned.1.call-done = bf16[256,1024]{1,0:T(8,128)(2,1)} async-done(((bf16[256,1024]{1,0:T(8,128)(2,1)}), bf16[256,1024]{1,0:T(8,128)(2,1)}) %all-reduce.8.cloned.1.call-update) | async-done | bytes 524304 | tf_op jit(solution)/shard_map/psum | solution.py:135
  264.3 48.7 %reduce-scatter.8.cloned.1.call-done = bf16[256,2176]{1,0:T(8,128)(2,1)} async-done(((bf16[1024,2176]{1,0:T(8,128)(2,1)}), bf16[256,2176]{1,0:T(8,128)(2,1)}) %reduce-scatter.8.cloned.1.call-update) | async-done | bytes 1114128 | tf_op jit(solution)/shard_map/reduce_scatter | solution.py:181
  313.0 1.1 fusion.36
  314.2 55.2 %all-reduce.10.cloned.1.call-done = bf16[256,2176]{1,0:T(8,128)(2,1)} async-done(((bf16[256,2176]{1,0:T(8,128)(2,1)}), bf16[256,2176]{1,0:T(8,128)(2,1)}) %all-reduce.10.cloned.1.call-update) | async-done | bytes 1114128 | tf_op jit(solution)/shard_map/psum | solution.py:181
  369.3 1.5 convert_element_type.87
  371.7 2.0 pad_maximum_fusion
  (113 shorter events, 14.6 us)
Async XLA Ops:
  7.2 7.7 %copy-start = (f32[16,49]{1,0:T(8,128)S(1)}, f32[16,49]{1,0:T(8,128)}, u32[]{:S(2)}) copy-start(f32[16,49]{1,0:T(8,128)} %param.20) | copy-start | bytes 9412
  7.2 7.1 %copy-start.5 = (bf16[8,16,1024]{2,1,0:T(8,128)(2,1)S(1)}, bf16[8,16,1024]{2,1,0:T(8,128)(2,1)}, u32[]{:S(2)}) copy-start(bf16[8,16,1024]{2,1,0:T(8,128)(2,1)} %param.15) | copy-start | bytes 786436
  7.2 7.4 %copy-start.18 = (f32[1024]{0:T(1024)S(1)}, f32[1024]{0:T(1024)}, u32[]{:S(2)}) copy-start(f32[1024]{0:T(1024)} %param.19) | copy-start | bytes 12292
  7.2 51.5 %all-gather.3.cloned.1.call-start = ((), (), s32[]{:S(2)}) async-start(), calls=%async_computation.3 | async-start | bytes 7864320 | tf_op jit(solution)/shard_map/all_gather | solution.py:70
  7.9 75.0 %all-gather.5.cloned.1.call-start = ((), (), s32[]{:S(2)}) async-start(), calls=%async_computation.4 | async-start | bytes 2621440 | tf_op jit(solution)/shard_map/all_gather | solution.py:71
  8.8 9.5 %collective-permute-start.4 = (s32[3,16]{1,0:T(4,128)S(1)}, s32[3,16]{1,0:T(4,128)S(1)}, u32[]{:S(2)}, u32[]{:S(2)}) collective-permute-start(s32[3,16]{1,0:T(4,128)S(1)} %get-tuple-element.76), channel_id=1, source_target_pairs={{0,4},{4,8},{8,12},{1,5},{5,9},{9,13},{2,6},{6,10},{10,14},{3,7},{... | collective-permute-start | bytes 584 | tf_op jit(solution)/shard_map/ppermute | solution.py:18
  11.1 7.1 %collective-permute-start.5 = (s32[3,16]{1,0:T(4,128)S(1)}, s32[3,16]{1,0:T(4,128)S(1)}, u32[]{:S(2)}, u32[]{:S(2)}) collective-permute-start(s32[3,16]{1,0:T(4,128)S(1)} %get-tuple-element.77), channel_id=1, source_target_pairs={{4,0},{8,4},{12,8},{5,1},{9,5},{13,9},{6,2},{10,6},{14,10},{7,3},{... | collective-permute-start | bytes 584 | tf_op jit(solution)/shard_map/ppermute | solution.py:19
  12.4 123.1 %reduce-scatter.4.cloned.1.call-start = ((), (), s32[]{:S(2)}) async-start(), calls=%async_computation.5 | async-start | bytes 2621440 | tf_op jit(solution)/shard_map/reduce_scatter | solution.py:104
  14.6 3.6 copy-start.17
  14.6 3.7 copy-start.15
  18.3 13.6 %collective-permute-start.6 = (s32[14,3]{1,0:T(8,128)S(1)}, s32[14,3]{1,0:T(8,128)S(1)}, u32[]{:S(2)}, u32[]{:S(2)}) collective-permute-start(s32[14,3]{1,0:T(8,128)S(1)} %get-tuple-element.74), channel_id=1, source_target_pairs={{0,1},{1,2},{2,3},{4,5},{5,6},{6,7},{8,9},{9,10},{10,11},{12,13},{... | collective-permute-start | bytes 512 | tf_op jit(solution)/shard_map/ppermute | solution.py:18
  22.6 9.3 %collective-permute-start.7 = (s32[14,3]{1,0:T(8,128)S(1)}, s32[14,3]{1,0:T(8,128)S(1)}, u32[]{:S(2)}, u32[]{:S(2)}) collective-permute-start(s32[14,3]{1,0:T(8,128)S(1)} %get-tuple-element.75), channel_id=1, source_target_pairs={{1,0},{2,1},{3,2},{5,4},{6,5},{7,6},{9,8},{10,9},{11,10},{13,12},{... | collective-permute-start | bytes 512 | tf_op jit(solution)/shard_map/ppermute | solution.py:19
  58.7 8.4 %copy-start.20 = (s32[128]{0:T(128)S(1)}, s32[128]{0:T(128)}, u32[]{:S(2)}) copy-start(s32[128]{0:T(128)} %iota.117) | copy-start | bytes 1540
  58.7 8.4 %copy-start.21 = (s32[128]{0:T(128)S(1)}, s32[128]{0:T(128)}, u32[]{:S(2)}) copy-start(s32[128]{0:T(128)} %iota.111) | copy-start | bytes 1540
  62.5 20.4 %copy-start.7 = (bf16[8,16,1024]{2,1,0:T(8,128)(2,1)S(1)}, bf16[8,16,1024]{2,1,0:T(8,128)(2,1)}, u32[]{:S(2)}) copy-start(bf16[8,16,1024]{2,1,0:T(8,128)(2,1)} %param.16) | copy-start | bytes 786436
  62.6 4.7 %collective-permute-start.1 = (bf16[3,16,2048]{2,1,0:T(8,128)(2,1)S(1)}, bf16[3,16,2048]{2,1,0:T(8,128)(2,1)S(1)}, u32[]{:S(2)}, u32[]{:S(2)}) collective-permute-start(bf16[3,16,2048]{2,1,0:T(8,128)(2,1)S(1)} %bitcast.78), channel_id=1, source_target_pairs={{4,0},{8,4},{12,8},{5,1},{9,5},{13,9},{6,2},{10,6},{14,10},{7,3},{... | collective-permute-start | bytes 589832 | tf_op jit(solution)/shard_map/ppermute | solution.py:19
  64.0 4.1 %collective-permute-start = (bf16[3,16,2048]{2,1,0:T(8,128)(2,1)S(1)}, bf16[3,16,2048]{2,1,0:T(8,128)(2,1)S(1)}, u32[]{:S(2)}, u32[]{:S(2)}) collective-permute-start(bf16[3,16,2048]{2,1,0:T(8,128)(2,1)S(1)} %bitcast.77), channel_id=1, source_target_pairs={{0,4},{4,8},{8,12},{1,5},{5,9},{9,13},{2,6},{6,10},{10,14},{3,7},{... | collective-permute-start | bytes 589832 | tf_op jit(solution)/shard_map/ppermute | solution.py:18
  69.1 18.0 %collective-permute-start.2 = (bf16[14,3,2048]{2,1,0:T(4,128)(2,1)}, bf16[14,3,2048]{2,1,0:T(4,128)(2,1)S(1)}, u32[]{:S(2)}, u32[]{:S(2)}) collective-permute-start(bf16[14,3,2048]{2,1,0:T(4,128)(2,1)} %get-tuple-element.68), channel_id=1, source_target_pairs={{0,1},{1,2},{2,3},{4,5},{5,6},{6,7},{8,9},{9,10},{10,11},{12,13},{... | collective-permute-start | bytes 516104 | tf_op jit(solution)/shard_map/ppermute | solution.py:18
  72.5 14.6 %collective-permute-start.3 = (bf16[14,3,2048]{2,1,0:T(4,128)(2,1)S(1)}, bf16[14,3,2048]{2,1,0:T(4,128)(2,1)}, u32[]{:S(2)}, u32[]{:S(2)}) collective-permute-start(bf16[14,3,2048]{2,1,0:T(4,128)(2,1)S(1)} %get-tuple-element.69), channel_id=1, source_target_pairs={{1,0},{2,1},{3,2},{5,4},{6,5},{7,6},{9,8},{10,9},{11,10},{13,12},{... | collective-permute-start | bytes 516104 | tf_op jit(solution)/shard_map/ppermute | solution.py:19
  96.7 5.2 %copy-start.2 = (f32[16,128,308]{1,2,0:T(8,128)}, f32[16,128,308]{1,2,0:T(8,128)S(1)}, u32[]{:S(2)}) copy-start(f32[16,128,308]{1,2,0:T(8,128)S(1)} %get-tuple-element.79) | copy-start | bytes 7569412
  96.7 1.7 copy-start.11
  96.7 2.0 copy-start.14
  101.8 74.3 %all-reduce.6.cloned.1.call-start = ((), (), s32[]{:S(2)}) async-start(), calls=%async_computation.6 | async-start | bytes 1048576 | tf_op jit(solution)/shard_map/psum | solution.py:103
  109.4 3.0 copy-start.10
  120.7 2.9 copy-start.4
  135.5 89.6 %reduce-scatter.6.cloned.1.call-start = ((), (), s32[]{:S(2)}) async-start(), calls=%async_computation.7 | async-start | bytes 2621440 | tf_op jit(solution)/shard_map/reduce_scatter | solution.py:135
  137.7 0.7 copy-start.8
  178.3 85.9 %all-reduce.8.cloned.1.call-start = ((), (), s32[]{:S(2)}) async-start(), calls=%async_computation.8 | async-start | bytes 1048576 | tf_op jit(solution)/shard_map/psum | solution.py:135
  180.7 12.9 %collective-permute-start.8 = (f32[3,22,2048]{2,1,0:T(8,128)}, f32[3,22,2048]{2,1,0:T(8,128)}, u32[]{:S(2)}, u32[]{:S(2)}) collective-permute-start(f32[3,22,2048]{2,1,0:T(8,128)} %get-tuple-element.65), channel_id=1, source_target_pairs={{0,4},{4,8},{8,12},{1,5},{5,9},{9,13},{2,6},{6,10},{10,14},{3,7},{... | collective-permute-start | bytes 1622024 | tf_op jit(solution)/shard_map/ppermute | solution.py:27
  182.8 12.1 %collective-permute-start.9 = (f32[3,22,2048]{2,1,0:T(8,128)}, f32[3,22,2048]{2,1,0:T(8,128)}, u32[]{:S(2)}, u32[]{:S(2)}) collective-permute-start(f32[3,22,2048]{2,1,0:T(8,128)} %get-tuple-element.64), channel_id=1, source_target_pairs={{4,0},{8,4},{12,8},{5,1},{9,5},{13,9},{6,2},{10,6},{14,10},{7,3},{... | collective-permute-start | bytes 1622024 | tf_op jit(solution)/shard_map/ppermute | solution.py:27
  194.9 5.6 %copy-start.6 = (f32[4,4,39424]{2,1,0:T(4,128)S(1)}, f32[4,4,39424]{2,1,0:T(4,128)}, u32[]{:S(2)}) copy-start(f32[4,4,39424]{2,1,0:T(4,128)} %dot_general.60) | copy-start | bytes 7569412
  196.4 7.6 %copy-start.9 = (bf16[16,64,128]{2,1,0:T(8,128)(2,1)S(1)}, bf16[16,64,128]{2,1,0:T(8,128)(2,1)}, u32[]{:S(2)}) copy-start(bf16[16,64,128]{2,1,0:T(8,128)(2,1)} %copy-done.8) | copy-start | bytes 786436
  197.4 10.5 %collective-permute-start.10 = (bf16[8,3,2048]{2,1,0:T(4,128)(2,1)}, bf16[8,3,2048]{2,1,0:T(4,128)(2,1)S(1)}, u32[]{:S(2)}, u32[]{:S(2)}) collective-permute-start(bf16[8,3,2048]{2,1,0:T(4,128)(2,1)} %get-tuple-element.71), channel_id=1, source_target_pairs={{0,1},{1,2},{2,3},{4,5},{5,6},{6,7},{8,9},{9,10},{10,11},{12,13},{... | collective-permute-start | bytes 294920 | tf_op jit(solution)/shard_map/ppermute | solution.py:27
  205.5 14.2 %copy-start.13 = (bf16[8,16,1024]{2,1,0:T(8,128)(2,1)S(1)}, bf16[8,16,1024]{2,1,0:T(8,128)(2,1)}, u32[]{:S(2)}) copy-start(bf16[8,16,1024]{2,1,0:T(8,128)(2,1)} %concatenate.45) | copy-start | bytes 786436
  205.5 14.2 %copy-start.16 = (f32[8,16]{1,0:T(8,128)S(1)}, f32[8,16]{1,0:T(8,128)}, u32[]{:S(2)}) copy-start(f32[8,16]{1,0:T(8,128)} %copy-done.15) | copy-start | bytes 1540
  205.5 14.2 %copy-start.19 = (f32[1024]{0:T(1024)S(1)}, f32[1024]{0:T(1024)}, u32[]{:S(2)}) copy-start(f32[1024]{0:T(1024)} %param.19) | copy-start | bytes 12292
  206.6 7.8 %collective-permute-start.11 = (bf16[8,3,2048]{2,1,0:T(4,128)(2,1)}, bf16[8,3,2048]{2,1,0:T(4,128)(2,1)S(1)}, u32[]{:S(2)}, u32[]{:S(2)}) collective-permute-start(bf16[8,3,2048]{2,1,0:T(4,128)(2,1)} %get-tuple-element.70), channel_id=1, source_target_pairs={{1,0},{2,1},{3,2},{5,4},{6,5},{7,6},{9,8},{10,9},{11,10},{13,12},{... | collective-permute-start | bytes 294920 | tf_op jit(solution)/shard_map/ppermute | solution.py:27
  225.2 87.8 %reduce-scatter.8.cloned.1.call-start = ((), (), s32[]{:S(2)}) async-start(), calls=%async_computation.9 | async-start | bytes 5570560 | tf_op jit(solution)/shard_map/reduce_scatter | solution.py:181
  264.2 49.8 %copy-start.12 = (bf16[256,1024]{1,0:T(8,128)(2,1)S(1)}, bf16[256,1024]{1,0:T(8,128)(2,1)}, u32[]{:S(2)}) copy-start(bf16[256,1024]{1,0:T(8,128)(2,1)} %all-reduce.8.cloned.1.call-done) | copy-start | bytes 1572868
  264.2 105.1 %all-reduce.10.cloned.1.call-start = ((), (), s32[]{:S(2)}) async-start(), calls=%async_computation.10 | async-start | bytes 2228224 | tf_op jit(solution)/shard_map/psum | solution.py:181
  369.3 2.2 copy-start.3
  371.5 2.9 copy-start.1
Sparse Core Ops, SparseCore 0:
  9.6 49.0 all-gather.2
  60.3 22.5 all-gather.4
  102.0 33.5 reduce-scatter.3
  137.8 38.2 all-reduce.5
  178.7 31.4 reduce-scatter.5
  225.3 38.8 all-reduce.7
  266.7 46.1 reduce-scatter.7
  315.4 53.8 all-reduce.9
where the time goes:
time: 382 us; the launch traced here: 381 us
  waiting for transfers between devices  224 us (59%)
  local copies, waits for them, and re-layouts  57.9 us (15%)
  matrix products  39.9 us (10%)
  starting transfers between devices  27.2 us (7%)
  other arithmetic  16.9 us (4%)
  between operations  14.8 us (4%)
    psum x1, waiting for transfers between devices, body(): lax.psum(lax.psum_scatter(big, 'row', scatter_dimension=0, tiled=True), '...  55.2 us
    reduce_scatter x1, waiting for transfers between devices, body(): lax.psum_scatter(big, 'row', scatter_dimension=0, tiled=True)  48.7 us
    psum x1, waiting for transfers between devices, body(): lax.psum(lax.psum_scatter(out_grad.astype(jnp.bfloat16), 'row', scatter_d...  35.6 us
    psum x1, waiting for transfers between devices, body(): lax.psum(lax.psum_scatter(query_term, 'row', scatter_dimension=0, tiled=T...  34.4 us
    all_gather x1, waiting for transfers between devices, body(): lax.all_gather(qkv_weight, 'row', axis=0, tiled=True)  26.6 us
    ppermute x4, starting transfers between devices, extended_2(): before = lax.ppermute(last, axis, up)  13.1 us
    reduce_scatter x1, waiting for transfers between devices, body(): lax.psum_scatter(out_grad.astype(jnp.bfloat16), 'row', scatter_dimension=...  10.7 us
    all_gather x1, waiting for transfers between devices, body(): lax.all_gather(out_weight, 'row', axis=0, tiled=True)  8.98 us
  transfers between devices with their start and end apart: 20, of which 9 were waited for; matrix products, arithmetic and copies ran while one was open for 24% of the time, Pallas kernels for 0%

commit v1 on v0

--- a/solution.py
+++ b/solution.py
@@ -128,11 +128,6 @@
         "hpk,phd->khd", probs, ag3.astype(jnp.float32), precision=HIGH,
         preferred_element_type=jnp.float32,
     )
-    query_term = jnp.dot(
-        flat.T, query_grad.reshape(nq, width).astype(jnp.bfloat16), preferred_element_type=jnp.float32
-    ).astype(jnp.bfloat16)
-    out_sum, query_term = lax.optimization_barrier((out_sum, query_term))
-    query_sum = lax.psum(lax.psum_scatter(query_term, "row", scatter_dimension=0, tiled=True), "col")
     buffer = jnp.concatenate(
         [key_ext_grad.reshape(ext_rows, ext_cols, width), value_ext_grad.reshape(ext_rows, ext_cols, width)],
         axis=-1,
@@ -171,18 +166,17 @@
     ).reshape(width, -1)
     offsets = bias_term.shape[1]
     spare = 128 - 1 - offsets
-    kv_pad = jnp.pad(joined_grad[:, width:], ((0, 0), (0, 128)))
-    big = jnp.dot(flat.T, kv_pad, preferred_element_type=jnp.float32).astype(jnp.bfloat16)
+    joined_pad = jnp.pad(joined_grad, ((0, 0), (0, 128)))
+    big = jnp.dot(flat.T, joined_pad, preferred_element_type=jnp.float32).astype(jnp.bfloat16)
     extra = jnp.concatenate(
         [gain_product[:, None], bias_rows, jnp.zeros((width, spare), jnp.float32)], axis=1
     ).astype(jnp.bfloat16)
-    big = lax.dynamic_update_slice_in_dim(big, extra, 2 * width, axis=1)
-    query_sum, big = lax.optimization_barrier((query_sum, big))
+    big = lax.dynamic_update_slice_in_dim(big, extra, 3 * width, axis=1)
     big_sum = lax.psum(lax.psum_scatter(big, "row", scatter_dimension=0, tiled=True), "col")
     big_sum = big_sum.astype(jnp.float32)
-    qkv_sum = jnp.concatenate([query_sum.astype(jnp.float32), big_sum[:, : 2 * width]], axis=1)
-    gain_sum = big_sum[:, 2 * width]
-    bias_sum = big_sum[:heads_per, 2 * width + 1 : 2 * width + 1 + offsets]
+    qkv_sum = big_sum[:, : 3 * width]
+    gain_sum = big_sum[:, 3 * width]
+    bias_sum = big_sum[:heads_per, 3 * width + 1 : 3 * width + 1 + offsets]
     return (patch_gradient, qkv_sum, out_sum, gain_sum, bias_sum)
 
 

time: 382 us -> 350 us (0.916)
  waiting for transfers between devices: 224 us -> 192 us
  local copies, waits for them, and re-layouts: 57.9 us -> 63.6 us
    psum x2 -> x0, waiting for transfers between devices: 70 us -> none  [the longest x1 35.6 us: body(): lax.psum(lax.psum_scatter(out_grad.astype(jnp.bfloat16), 'row', scatter_d...]
    psum x1, waiting for transfers between devices: 55.2 us -> 90.8 us  [body(): lax.psum(lax.psum_scatter(big, 'row', scatter_dimension=0, tiled=True), '...]
    reduce_scatter x1, waiting for transfers between devices: 48.7 us -> 62 us  [body(): lax.psum_scatter(big, 'row', scatter_dimension=0, tiled=True)]
    reduce_scatter x1, waiting for transfers between devices: 10.7 us -> 0.02 us  [body(): lax.psum_scatter(out_grad.astype(jnp.bfloat16), 'row', scatter_dimension=...]
    slice x3, local copies, waits for them, and re-layouts: 1.56 us -> 5.56 us  [the longest x1 3.56 us: body(): qkv_sum = big_sum[:, :3 * width]]
    unnamed x47 -> x65, local copies, waits for them, and re-layouts: 7.62 us -> 8.82 us
  transfers between devices with their start and end apart: 20 -> 17, of which waited for: 9 -> 6; matrix products, arithmetic and copies ran while one was open for 24% -> 19% of each run, Pallas kernels for 0% -> 0%
where the time goes in v1:
time: 350 us; the launch traced here: 349 us
  waiting for transfers between devices  192 us (55%)
  local copies, waits for them, and re-layouts  63.6 us (18%)
  matrix products  37.2 us (11%)
  starting transfers between devices  28.8 us (8%)
  between operations  14.4 us (4%)
  other arithmetic  13.4 us (4%)
    psum x1, waiting for transfers between devices, body(): lax.psum(lax.psum_scatter(big, 'row', scatter_dimension=0, tiled=True), '...  90.8 us
    reduce_scatter x1, waiting for transfers between devices, body(): lax.psum_scatter(big, 'row', scatter_dimension=0, tiled=True)  62 us
    all_gather x1, waiting for transfers between devices, body(): lax.all_gather(qkv_weight, 'row', axis=0, tiled=True)  25.4 us
    ppermute x4, starting transfers between devices, extended_2(): before = lax.ppermute(last, axis, up)  13.8 us
    ppermute x4, starting transfers between devices, passed_along(): lax.ppermute(value, axis, [(source, source + steps) for source in range(f...  9.46 us
    unnamed x65, local copies, waits for them, and re-layouts  8.82 us
    all_gather x1, waiting for transfers between devices, body(): lax.all_gather(out_weight, 'row', axis=0, tiled=True)  8.16 us
  transfers between devices with their start and end apart: 17, of which 6 were waited for; matrix products, arithmetic and copies ran while one was open for 19% of the time, Pallas kernels for 0%

profile of v1, /device:TPU:0, one launch (start us, length us, event | category | flops | bytes accessed | tf_op | source)
XLA Modules:
  0.0 349.2 jit_solution(665185740647419891)
XLA Ops:
  8.0 0.8 fusion.64
  8.8 2.3 collective-permute-start.4
  11.1 1.3 collective-permute-start.5
  14.6 0.9 fusion.39
  15.6 3.1 convolution_bitcast_fusion
  20.2 4.3 %collective-permute-start.6 = (s32[14,3]{1,0:T(8,128)S(1)}, s32[14,3]{1,0:T(8,128)S(1)}, u32[]{:S(2)}, u32[]{:S(2)}) collective-permute-start(s32[14,3]{1,0:T(8,128)S(1)} %get-tuple-element.68), channel_id=1, source_target_pairs={{0,1},{1,2},{2,3},{4,5},{5,6},{6,7},{8,9},{9,10},{10,11},{12,13},{... | collective-permute-start | bytes 512 | tf_op jit(solution)/shard_map/ppermute | solution.py:18
  24.5 1.3 collective-permute-start.7
  25.8 4.5 %reshape.400 = f32[16,128,308]{2,1,0:T(8,128)} reshape(f32[16,39424]{1,0:T(8,128)S(1)} %convolution_bitcast_fusion) | data formatting | bytes 5046272 | tf_op jit(solution)/shard_map/reshape | solution.py:88
  30.3 2.4 copy.25
  33.4 25.4 %all-gather.3.cloned.1.call-done = bf16[1024,3072]{1,0:T(8,128)(2,1)} async-done(((bf16[256,3072]{1,0:T(8,128)(2,1)}), bf16[1024,3072]{1,0:T(8,128)(2,1)}) %all-gather.3.cloned.1.call-update) | async-done | bytes 6291472 | tf_op jit(solution)/shard_map/all_gather | solution.py:70
  58.7 3.9 %convolution_convert_fusion.1 = bf16[128,3072]{1,0:T(8,128)(2,1)S(1)} fusion(bf16[128,1024]{1,0:T(8,128)(2,1)} %bitcast.59, bf16[1024,3072]{1,0:T(8,128)(2,1)} %all-gather.3.cloned.1.call-done), kind=kOutput, calls=%fused_computation.9 | convolution fusion | flops 805699584 | bytes 7340032 | tf_op jit(solution)/shard_map/dot_general | solution.py:77
  62.7 1.3 collective-permute-start.1
  64.0 3.0 collective-permute-start
  68.1 1.0 pad_maximum_fusion.3
  69.2 4.1 %collective-permute-start.2 = (bf16[14,3,2048]{2,1,0:T(4,128)(2,1)}, bf16[14,3,2048]{2,1,0:T(4,128)(2,1)}, u32[]{:S(2)}, u32[]{:S(2)}) collective-permute-start(bf16[14,3,2048]{2,1,0:T(4,128)(2,1)} %get-tuple-element.62), channel_id=1, source_target_pairs={{0,1},{1,2},{2,3},{4,5},{5,6},{6,7},{8,9},{9,10},{10,11},{12,13},{... | collective-permute-start | bytes 516104 | tf_op jit(solution)/shard_map/ppermute | solution.py:18
  73.3 1.5 collective-permute-start.3
  74.7 8.2 %all-gather.5.cloned.1.call-done = bf16[1024,1024]{1,0:T(8,128)(2,1)} async-done(((bf16[256,1024]{1,0:T(8,128)(2,1)}), bf16[1024,1024]{1,0:T(8,128)(2,1)}) %all-gather.5.cloned.1.call-update) | async-done | bytes 2097168 | tf_op jit(solution)/shard_map/all_gather | solution.py:71
  82.9 3.2 convolution_convert_fusion.4
  86.1 1.8 copy.26
  88.7 1.8 copy.24
  90.4 3.1 pad_maximum_fusion
  93.5 2.4 reshape.397
  95.9 2.4 fusion.60
  98.3 1.4 copy.34
  99.8 2.2 copy.35
  102.0 1.8 fusion.65
  105.0 1.8 multiply_reduce_fusion
  106.8 2.4 convolution_bitcast_fusion.1
  109.2 0.9 subtract_multiply_fusion
  110.1 3.2 copy.30
  113.3 3.0 reshape.405
  116.3 3.1 multiply_bitcast_fusion
  119.4 3.2 copy.29
  122.5 3.0 reshape.404
  125.5 1.5 constant_dynamic-update-slice_fusion.1
  127.4 1.6 copy-done.3
  129.0 1.1 fusion.59
  130.1 2.9 collective-permute-start.8
  133.1 2.1 convolution_convert_fusion.2
  135.8 1.5 collective-permute-start.9
  137.3 1.5 fusion.11
  138.8 2.3 copy.32
  141.1 1.8 slice.206
  142.9 5.5 %dot_general.55 = f32[4,4,39424]{2,1,0:T(4,128)} reshape(f32[16,128,308]{2,1,0:T(8,128)} %copy.32) | data formatting | bytes 5046272 | tf_op jit(solution)/shard_map/dot_general | solution.py:115
  148.4 1.3 fusion.38
  149.8 1.4 fusion.37
  151.3 0.8 fusion.61
  152.1 3.7 %collective-permute-start.10 = (bf16[8,3,2048]{2,1,0:T(4,128)(2,1)S(1)}, bf16[8,3,2048]{2,1,0:T(4,128)(2,1)}, u32[]{:S(2)}, u32[]{:S(2)}) collective-permute-start(bf16[8,3,2048]{2,1,0:T(4,128)(2,1)S(1)} %get-tuple-element.65), channel_id=1, source_target_pairs={{0,1},{1,2},{2,3},{4,5},{5,6},{6,7},{8,9},{9,10},{10,11},{12,13},{... | collective-permute-start | bytes 294920 | tf_op jit(solution)/shard_map/ppermute | solution.py:27
  155.8 3.4 fusion.12
  159.8 1.1 concatenate.46
  161.7 1.3 collective-permute-start.11
  163.0 1.0 slice_add_fusion.3
  164.0 0.8 scatter-add.16
  164.8 4.1 %collective-permute-done.11 = bf16[8,3,2048]{2,1,0:T(4,128)(2,1)S(1)} collective-permute-done((bf16[8,3,2048]{2,1,0:T(4,128)(2,1)}, bf16[8,3,2048]{2,1,0:T(4,128)(2,1)S(1)}, u32[]{:S(2)}, u32[]{:S(2)}) %collective-permute-start.11) | collective-permute-done | bytes 98336 | tf_op jit(solution)/shard_map/ppermute | solution.py:27
  169.9 5.2 %fusion.44 = (bf16[1024]{0:T(1024)(128)(2,1)S(1)}, f32[8,16]{1,0:T(8,128)S(1)}, f32[8,16]{1,0:T(8,128)S(1)}, f32[8,16,1024]{2,1,0:T(8,128)S(1)}) fusion(bf16[8,16,1024]{2,1,0:T(8,128)(2,1)S(1)} %copy-done.8, f32[8,16]{1,0:T(8,128)S(1)} %copy-done.21, f32[8,16]{1,0:T(8,128)S(1)} %broadcast_multiply_fusion.2, f32[1024]{0:T(1024)S(1)} %copy-done.24, ...), kind=kOutput, calls=%fused_computation.61 | convolution fusion | flops 808057600 | bytes 7872512 | tf_op jit(solution)/shard_map/dot_general | solution.py:151
  175.4 4.7 %convolution_convert_fusion = bf16[1024,3200]{1,0:T(8,128)(2,1)} fusion(bf16[128,1024]{1,0:T(8,128)(2,1)S(1)} %bitcast.60, bf16[128,2048]{1,0:T(8,128)(2,1)S(1)} %bitcast.67, bf16[128,1024]{1,0:T(8,128)(2,1)S(1)} %copy.31), kind=kOutput, calls=%fused_computation.4 | convolution fusion | flops 845004800 | bytes 7602176 | tf_op jit(solution)/shard_map/dot_general | solution.py:170
  180.1 0.9 maximum_dynamic-update-slice_fusion
  181.1 62.0 %reduce-scatter.3.cloned.1.call-done = bf16[256,3200]{1,0:T(8,128)(2,1)} async-done(((bf16[1024,3200]{1,0:T(8,128)(2,1)}), bf16[256,3200]{1,0:T(8,128)(2,1)}) %reduce-scatter.3.cloned.1.call-update) | async-done | bytes 1638416 | tf_op jit(solution)/shard_map/reduce_scatter | solution.py:175
  243.2 1.1 fusion.43
  244.2 90.8 %all-reduce.5.cloned.1.call-done = (bf16[256,3200]{1,0:T(8,128)(2,1)}, bf16[256,1024]{1,0:T(8,128)(2,1)}) async-done(((bf16[256,3200]{1,0:T(8,128)(2,1)}, bf16[256,1024]{1,0:T(8,128)(2,1)}), (bf16[256,3200]{1,0:T(8,128)(2,1)}, bf16[256,1024]{1,0:T(8,128)(2,1)})) %all-reduce.5.cloned.1.call-update) | async-done | bytes 2162704 | tf_op jit(solution)/shard_map/psum | solution.py:175
  335.0 1.3 slice.218
  336.3 3.6 %slice.216 = f32[256,3072]{1,0:T(8,128)} slice(bf16[256,3200]{1,0:T(8,128)(2,1)} %get-tuple-element.56), slice={[0:256], [0:3072]} | slice | bytes 6291456 | tf_op jit(solution)/shard_map/slice | solution.py:177
  340.1 0.8 copy-done.17
  340.9 1.1 convert_element_type.74
  (120 shorter events, 12.7 us)
Async XLA Ops:
  7.2 8.4 %copy-start = (f32[16,49]{1,0:T(8,128)S(1)}, f32[16,49]{1,0:T(8,128)}, u32[]{:S(2)}) copy-start(f32[16,49]{1,0:T(8,128)} %param.20) | copy-start | bytes 9412
  7.2 7.1 %copy-start.7 = (bf16[8,16,1024]{2,1,0:T(8,128)(2,1)S(1)}, bf16[8,16,1024]{2,1,0:T(8,128)(2,1)}, u32[]{:S(2)}) copy-start(bf16[8,16,1024]{2,1,0:T(8,128)(2,1)} %param.15) | copy-start | bytes 786436
  7.2 7.4 %copy-start.23 = (f32[1024]{0:T(1024)S(1)}, f32[1024]{0:T(1024)}, u32[]{:S(2)}) copy-start(f32[1024]{0:T(1024)} %param.19) | copy-start | bytes 12292
  7.2 51.5 %all-gather.3.cloned.1.call-start = ((), (), s32[]{:S(2)}) async-start(), calls=%async_computation.2 | async-start | bytes 7864320 | tf_op jit(solution)/shard_map/all_gather | solution.py:70
  7.9 75.0 %all-gather.5.cloned.1.call-start = ((), (), s32[]{:S(2)}) async-start(), calls=%async_computation.3 | async-start | bytes 2621440 | tf_op jit(solution)/shard_map/all_gather | solution.py:71
  8.8 11.3 %collective-permute-start.4 = (s32[3,16]{1,0:T(4,128)S(1)}, s32[3,16]{1,0:T(4,128)S(1)}, u32[]{:S(2)}, u32[]{:S(2)}) collective-permute-start(s32[3,16]{1,0:T(4,128)S(1)} %get-tuple-element.70), channel_id=1, source_target_pairs={{0,4},{4,8},{8,12},{1,5},{5,9},{9,13},{2,6},{6,10},{10,14},{3,7},{... | collective-permute-start | bytes 584 | tf_op jit(solution)/shard_map/ppermute | solution.py:18
  11.1 9.0 %collective-permute-start.5 = (s32[3,16]{1,0:T(4,128)S(1)}, s32[3,16]{1,0:T(4,128)S(1)}, u32[]{:S(2)}, u32[]{:S(2)}) collective-permute-start(s32[3,16]{1,0:T(4,128)S(1)} %get-tuple-element.71), channel_id=1, source_target_pairs={{4,0},{8,4},{12,8},{5,1},{9,5},{13,9},{6,2},{10,6},{14,10},{7,3},{... | collective-permute-start | bytes 584 | tf_op jit(solution)/shard_map/ppermute | solution.py:19
  12.4 168.6 %reduce-scatter.5.cloned.1.call-start = ((), (), s32[]{:S(2)}) async-start(), calls=%async_computation.5 | async-start | bytes 2621440 | tf_op jit(solution)/shard_map/reduce_scatter | solution.py:104
  14.6 5.5 %copy-start.22 = (s32[8,16]{1,0:T(8,128)S(1)}, s32[8,16]{1,0:T(8,128)}, u32[]{:S(2)}) copy-start(s32[8,16]{1,0:T(8,128)} %param.21) | copy-start | bytes 1540
  14.6 5.5 %copy-start.20 = (f32[8,16]{1,0:T(8,128)}, f32[8,16]{1,0:T(8,128)S(1)}, u32[]{:S(2)}) copy-start(f32[8,16]{1,0:T(8,128)S(1)} %add_rsqrt_fusion) | copy-start | bytes 1540
  20.2 12.5 %collective-permute-start.6 = (s32[14,3]{1,0:T(8,128)S(1)}, s32[14,3]{1,0:T(8,128)S(1)}, u32[]{:S(2)}, u32[]{:S(2)}) collective-permute-start(s32[14,3]{1,0:T(8,128)S(1)} %get-tuple-element.68), channel_id=1, source_target_pairs={{0,1},{1,2},{2,3},{4,5},{5,6},{6,7},{8,9},{9,10},{10,11},{12,13},{... | collective-permute-start | bytes 512 | tf_op jit(solution)/shard_map/ppermute | solution.py:18
  24.5 8.2 %collective-permute-start.7 = (s32[14,3]{1,0:T(8,128)S(1)}, s32[14,3]{1,0:T(8,128)S(1)}, u32[]{:S(2)}, u32[]{:S(2)}) collective-permute-start(s32[14,3]{1,0:T(8,128)S(1)} %get-tuple-element.69), channel_id=1, source_target_pairs={{1,0},{2,1},{3,2},{5,4},{6,5},{7,6},{9,8},{10,9},{11,10},{13,12},{... | collective-permute-start | bytes 512 | tf_op jit(solution)/shard_map/ppermute | solution.py:19
  58.7 8.3 %copy-start.25 = (s32[308]{0:T(512)S(1)}, s32[308]{0:T(512)}, u32[]{:S(2)}) copy-start(s32[308]{0:T(512)} %iota.114) | copy-start | bytes 3700
  58.7 8.3 %copy-start.26 = (s32[308]{0:T(512)S(1)}, s32[308]{0:T(512)}, u32[]{:S(2)}) copy-start(s32[308]{0:T(512)} %iota.108) | copy-start | bytes 3700
  58.7 8.4 %copy-start.27 = (s32[128]{0:T(128)S(1)}, s32[128]{0:T(128)}, u32[]{:S(2)}) copy-start(s32[128]{0:T(128)} %iota.117) | copy-start | bytes 1540
  58.7 8.4 %copy-start.28 = (s32[128]{0:T(128)S(1)}, s32[128]{0:T(128)}, u32[]{:S(2)}) copy-start(s32[128]{0:T(128)} %iota.111) | copy-start | bytes 1540
  58.7 8.4 %copy-start.29 = (pred[308]{0:T(512)(128)(4,1)S(1)}, pred[308]{0:T(512)(128)(4,1)}, u32[]{:S(2)}) copy-start(pred[308]{0:T(512)(128)(4,1)} %eq.44) | copy-start | bytes 928
  62.7 4.7 %collective-permute-start.1 = (bf16[3,16,2048]{2,1,0:T(8,128)(2,1)S(1)}, bf16[3,16,2048]{2,1,0:T(8,128)(2,1)S(1)}, u32[]{:S(2)}, u32[]{:S(2)}) collective-permute-start(bf16[3,16,2048]{2,1,0:T(8,128)(2,1)S(1)} %bitcast.75), channel_id=1, source_target_pairs={{4,0},{8,4},{12,8},{5,1},{9,5},{13,9},{6,2},{10,6},{14,10},{7,3},{... | collective-permute-start | bytes 589832 | tf_op jit(solution)/shard_map/ppermute | solution.py:19
  64.0 4.1 %collective-permute-start = (bf16[3,16,2048]{2,1,0:T(8,128)(2,1)S(1)}, bf16[3,16,2048]{2,1,0:T(8,128)(2,1)S(1)}, u32[]{:S(2)}, u32[]{:S(2)}) collective-permute-start(bf16[3,16,2048]{2,1,0:T(8,128)(2,1)S(1)} %bitcast.74), channel_id=1, source_target_pairs={{0,4},{4,8},{8,12},{1,5},{5,9},{9,13},{2,6},{6,10},{10,14},{3,7},{... | collective-permute-start | bytes 589832 | tf_op jit(solution)/shard_map/ppermute | solution.py:18
  67.3 0.8 copy-start.5
  67.4 1.8 copy-start.15
  68.1 1.1 copy-start.16
  69.2 21.3 %collective-permute-start.2 = (bf16[14,3,2048]{2,1,0:T(4,128)(2,1)}, bf16[14,3,2048]{2,1,0:T(4,128)(2,1)}, u32[]{:S(2)}, u32[]{:S(2)}) collective-permute-start(bf16[14,3,2048]{2,1,0:T(4,128)(2,1)} %get-tuple-element.62), channel_id=1, source_target_pairs={{0,1},{1,2},{2,3},{4,5},{5,6},{6,7},{8,9},{9,10},{10,11},{12,13},{... | collective-permute-start | bytes 516104 | tf_op jit(solution)/shard_map/ppermute | solution.py:18
  73.3 17.2 %collective-permute-start.3 = (bf16[14,3,2048]{2,1,0:T(4,128)(2,1)}, bf16[14,3,2048]{2,1,0:T(4,128)(2,1)}, u32[]{:S(2)}, u32[]{:S(2)}) collective-permute-start(bf16[14,3,2048]{2,1,0:T(4,128)(2,1)} %get-tuple-element.63), channel_id=1, source_target_pairs={{1,0},{2,1},{3,2},{5,4},{6,5},{7,6},{9,8},{10,9},{11,10},{13,12},{... | collective-permute-start | bytes 516104 | tf_op jit(solution)/shard_map/ppermute | solution.py:19
  103.8 1.1 copy-start.14
  103.9 1.2 copy-start.19
  125.5 1.8 copy-start.4
  127.3 5.8 %copy-start.10 = (bf16[8,16,1024]{2,1,0:T(8,128)(2,1)S(1)}, bf16[8,16,1024]{2,1,0:T(8,128)(2,1)}, u32[]{:S(2)}) copy-start(bf16[8,16,1024]{2,1,0:T(8,128)(2,1)} %param.16) | copy-start | bytes 786436
  127.3 5.8 %copy-start.18 = (bf16[16,64,128]{2,1,0:T(8,128)(2,1)S(1)}, bf16[16,64,128]{2,1,0:T(8,128)(2,1)}, u32[]{:S(2)}) copy-start(bf16[16,64,128]{2,1,0:T(8,128)(2,1)} %get-tuple-element.75) | copy-start | bytes 786436
  127.4 1.6 copy-start.3
  130.1 18.3 %collective-permute-start.8 = (f32[3,22,2048]{2,1,0:T(8,128)}, f32[3,22,2048]{2,1,0:T(8,128)}, u32[]{:S(2)}, u32[]{:S(2)}) collective-permute-start(f32[3,22,2048]{2,1,0:T(8,128)} %get-tuple-element.59), channel_id=1, source_target_pairs={{0,4},{4,8},{8,12},{1,5},{5,9},{9,13},{2,6},{6,10},{10,14},{3,7},{... | collective-permute-start | bytes 1622024 | tf_op jit(solution)/shard_map/ppermute | solution.py:27
  135.2 108.0 %reduce-scatter.3.cloned.1.call-start = ((), (), s32[]{:S(2)}) async-start(), calls=%async_computation.4 | async-start | bytes 8192000 | tf_op jit(solution)/shard_map/reduce_scatter | solution.py:175
  135.8 13.9 %collective-permute-start.9 = (f32[3,22,2048]{2,1,0:T(8,128)}, f32[3,22,2048]{2,1,0:T(8,128)}, u32[]{:S(2)}, u32[]{:S(2)}) collective-permute-start(f32[3,22,2048]{2,1,0:T(8,128)} %get-tuple-element.58), channel_id=1, source_target_pairs={{4,0},{8,4},{12,8},{5,1},{9,5},{13,9},{6,2},{10,6},{14,10},{7,3},{... | collective-permute-start | bytes 1622024 | tf_op jit(solution)/shard_map/ppermute | solution.py:27
  149.8 6.0 %copy-start.9 = (f32[4,4,39424]{2,1,0:T(4,128)S(1)}, f32[4,4,39424]{2,1,0:T(4,128)}, u32[]{:S(2)}) copy-start(f32[4,4,39424]{2,1,0:T(4,128)} %dot_general.55) | copy-start | bytes 7569412
  151.1 8.1 %copy-start.12 = (bf16[16,64,128]{2,1,0:T(8,128)(2,1)S(1)}, bf16[16,64,128]{2,1,0:T(8,128)(2,1)}, u32[]{:S(2)}) copy-start(bf16[16,64,128]{2,1,0:T(8,128)(2,1)} %fusion.11) | copy-start | bytes 786436
  152.1 11.0 %collective-permute-start.10 = (bf16[8,3,2048]{2,1,0:T(4,128)(2,1)S(1)}, bf16[8,3,2048]{2,1,0:T(4,128)(2,1)}, u32[]{:S(2)}, u32[]{:S(2)}) collective-permute-start(bf16[8,3,2048]{2,1,0:T(4,128)(2,1)S(1)} %get-tuple-element.65), channel_id=1, source_target_pairs={{0,1},{1,2},{2,3},{4,5},{5,6},{6,7},{8,9},{9,10},{10,11},{12,13},{... | collective-permute-start | bytes 294920 | tf_op jit(solution)/shard_map/ppermute | solution.py:27
  161.6 8.2 %copy-start.8 = (bf16[8,16,1024]{2,1,0:T(8,128)(2,1)S(1)}, bf16[8,16,1024]{2,1,0:T(8,128)(2,1)}, u32[]{:S(2)}) copy-start(bf16[8,16,1024]{2,1,0:T(8,128)(2,1)} %param.15) | copy-start | bytes 786436
  161.6 8.2 %copy-start.21 = (f32[8,16]{1,0:T(8,128)S(1)}, f32[8,16]{1,0:T(8,128)}, u32[]{:S(2)}) copy-start(f32[8,16]{1,0:T(8,128)} %copy-done.20) | copy-start | bytes 1540
  161.6 8.3 %copy-start.24 = (f32[1024]{0:T(1024)S(1)}, f32[1024]{0:T(1024)}, u32[]{:S(2)}) copy-start(f32[1024]{0:T(1024)} %param.19) | copy-start | bytes 12292
  161.7 7.2 %collective-permute-start.11 = (bf16[8,3,2048]{2,1,0:T(4,128)(2,1)}, bf16[8,3,2048]{2,1,0:T(4,128)(2,1)S(1)}, u32[]{:S(2)}, u32[]{:S(2)}) collective-permute-start(bf16[8,3,2048]{2,1,0:T(4,128)(2,1)} %get-tuple-element.64), channel_id=1, source_target_pairs={{1,0},{2,1},{3,2},{5,4},{6,5},{7,6},{9,8},{10,9},{11,10},{13,12},{... | collective-permute-start | bytes 294920 | tf_op jit(solution)/shard_map/ppermute | solution.py:27
  169.9 5.5 %copy-start.6 = (bf16[8,16,1024]{2,1,0:T(8,128)(2,1)S(1)}, bf16[8,16,1024]{2,1,0:T(8,128)(2,1)}, u32[]{:S(2)}) copy-start(bf16[8,16,1024]{2,1,0:T(8,128)(2,1)} %fusion.39) | copy-start | bytes 786436
  175.4 4.7 %copy-start.13 = (bf16[4,256,49]{2,1,0:T(8,128)(2,1)S(1)}, bf16[4,256,49]{2,1,0:T(8,128)(2,1)}, u32[]{:S(2)}) copy-start(bf16[4,256,49]{2,1,0:T(8,128)(2,1)} %pad.18) | copy-start | bytes 301060
  175.4 4.7 %copy-start.30 = (bf16[128]{0:T(256)(128)(2,1)S(1)}, bf16[128]{0:T(256)(128)(2,1)}, u32[]{:S(2)}) copy-start(bf16[128]{0:T(256)(128)(2,1)} %pad.21.clone) | copy-start | bytes 772
  181.0 62.2 %copy-start.11 = (bf16[8,16,1024]{2,1,0:T(8,128)(2,1)S(1)}, bf16[8,16,1024]{2,1,0:T(8,128)(2,1)}, u32[]{:S(2)}) copy-start(bf16[8,16,1024]{2,1,0:T(8,128)(2,1)} %param.16) | copy-start | bytes 786436
  181.0 154.0 %all-reduce.5.cloned.1.call-start = ((), (), s32[]{:S(2)}) async-start(), calls=%async_computation.6 | async-start | bytes 4325376 | tf_op jit(solution)/shard_map/psum | solution.py:175
  336.3 3.6 %copy-start.2 = (bf16[256,3200]{1,0:T(8,128)(2,1)S(1)}, bf16[256,3200]{1,0:T(8,128)(2,1)}, u32[]{:S(2)}) copy-start(bf16[256,3200]{1,0:T(8,128)(2,1)} %get-tuple-element.56) | copy-start | bytes 4915204
  336.3 6.4 %copy-start.1 = (f32[16,49]{1,0:T(8,128)S(1)}, f32[16,49]{1,0:T(8,128)}, u32[]{:S(2)}) copy-start(f32[16,49]{1,0:T(8,128)} %param.20) | copy-start | bytes 9412
  339.9 1.0 copy-start.17
Sparse Core Ops, SparseCore 0:
  9.6 49.0 all-gather.2
  60.3 22.5 all-gather.4
  135.3 32.8 reduce-scatter.4
  181.1 61.9 reduce-scatter.2
  245.4 89.5 all-reduce.4

commit v2 on v1

--- a/solution.py
+++ b/solution.py
@@ -25,6 +25,11 @@
     count = lax.axis_size(axis)
     first, last = (max(0, -steps), min(count, count - steps))
     return lax.ppermute(value, axis, [(source, source + steps) for source in range(first, last)])
+
+
+def col_all_reduce(value):
+    part = lax.psum_scatter(lax.optimization_barrier(value), "col", scatter_dimension=0, tiled=True)
+    return lax.all_gather(part, "col", axis=0, tiled=True)
 
 
 def apply_layer_norm(values, norm_gain_value):
@@ -100,8 +105,8 @@
 
     grad_flat = upstream.reshape(-1, width)
     out_grad = jnp.dot(attended.T, grad_flat, preferred_element_type=jnp.float32)
-    out_sum = lax.psum(
-        lax.psum_scatter(out_grad.astype(jnp.bfloat16), "row", scatter_dimension=0, tiled=True), "col"
+    out_sum = col_all_reduce(
+        lax.psum_scatter(out_grad.astype(jnp.bfloat16), "row", scatter_dimension=0, tiled=True)
     ).astype(jnp.float32)
     attended_grad = jnp.dot(grad_flat, full_out.T, preferred_element_type=jnp.float32).astype(
         jnp.bfloat16
@@ -172,7 +177,7 @@
         [gain_product[:, None], bias_rows, jnp.zeros((width, spare), jnp.float32)], axis=1
     ).astype(jnp.bfloat16)
     big = lax.dynamic_update_slice_in_dim(big, extra, 3 * width, axis=1)
-    big_sum = lax.psum(lax.psum_scatter(big, "row", scatter_dimension=0, tiled=True), "col")
+    big_sum = col_all_reduce(lax.psum_scatter(big, "row", scatter_dimension=0, tiled=True))
     big_sum = big_sum.astype(jnp.float32)
     qkv_sum = big_sum[:, : 3 * width]
     gain_sum = big_sum[:, 3 * width]

time: 350 us -> 389 us (1.11)
  waiting for transfers between devices: 192 us -> 213 us
  blocking collectives: 0 us -> 18.6 us
    psum x1 -> x0, waiting for transfers between devices: 90.8 us -> none  [body(): lax.psum(lax.psum_scatter(big, 'row', scatter_dimension=0, tiled=True), '...]
    reduce_scatter x0 -> x2, waiting for transfers between devices: none -> 60.2 us  [col_all_reduce(): lax.psum_scatter(lax.optimization_barrier(value), 'col', scatter_dimensio...]
    reduce_scatter x1, waiting for transfers between devices: 0.02 us -> 34.5 us  [body(): lax.psum_scatter(out_grad.astype(jnp.bfloat16), 'row', scatter_dimension=...]
    all_gather x0 -> x1, waiting for transfers between devices: none -> 19.8 us  [col_all_reduce(): return lax.all_gather(part, 'col', axis=0, tiled=True)]
    all_gather x0 -> x1, blocking collectives: none -> 18.6 us  [col_all_reduce(): return lax.all_gather(part, 'col', axis=0, tiled=True)]
    unnamed x65 -> x61, local copies, waits for them, and re-layouts: 8.82 us -> 8.94 us
  transfers between devices with their start and end apart: 17 -> 19, of which waited for: 6 -> 9; matrix products, arithmetic and copies ran while one was open for 19% -> 14% of each run, Pallas kernels for 0% -> 0%
where the time goes in v2:
time: 389 us; the launch traced here: 388 us
  waiting for transfers between devices  213 us (55%)
  local copies, waits for them, and re-layouts  61.1 us (16%)
  matrix products  37.1 us (10%)
  starting transfers between devices  29.3 us (8%)
  blocking collectives  18.6 us (5%)
  other arithmetic  14.9 us (4%)
  between operations  14.7 us (4%)
    reduce_scatter x2, waiting for transfers between devices, col_all_reduce(): lax.psum_scatter(lax.optimization_barrier(value), 'col', scatter_dimensio...  60.2 us
    reduce_scatter x1, waiting for transfers between devices, body(): lax.psum_scatter(big, 'row', scatter_dimension=0, tiled=True)  58.7 us
    reduce_scatter x1, waiting for transfers between devices, body(): lax.psum_scatter(out_grad.astype(jnp.bfloat16), 'row', scatter_dimension=...  34.5 us
    all_gather x1, waiting for transfers between devices, body(): lax.all_gather(qkv_weight, 'row', axis=0, tiled=True)  25.4 us
    all_gather x1, waiting for transfers between devices, col_all_reduce(): return lax.all_gather(part, 'col', axis=0, tiled=True)  19.8 us
    all_gather x1, blocking collectives, col_all_reduce(): return lax.all_gather(part, 'col', axis=0, tiled=True)  18.6 us
    ppermute x4, starting transfers between devices, extended_2(): before = lax.ppermute(last, axis, up)  13.8 us
    ppermute x4, starting transfers between devices, passed_along(): lax.ppermute(value, axis, [(source, source + steps) for source in range(f...  9.83 us
  transfers between devices with their start and end apart: 19, of which 9 were waited for; matrix products, arithmetic and copies ran while one was open for 14% of the time, Pallas kernels for 0%

profile of v2, /device:TPU:0, one launch (start us, length us, event | category | flops | bytes accessed | tf_op | source)
XLA Modules:
  0.0 388.2 jit_solution(14441056066647982945)
XLA Ops:
  8.8 2.3 collective-permute-start.4
  11.1 1.3 collective-permute-start.5
  14.6 0.9 fusion.39
  15.6 3.1 convolution_bitcast_fusion
  20.1 4.3 %collective-permute-start.6 = (s32[14,3]{1,0:T(8,128)S(1)}, s32[14,3]{1,0:T(8,128)S(1)}, u32[]{:S(2)}, u32[]{:S(2)}) collective-permute-start(s32[14,3]{1,0:T(8,128)S(1)} %get-tuple-element.66), channel_id=1, source_target_pairs={{0,1},{1,2},{2,3},{4,5},{5,6},{6,7},{8,9},{9,10},{10,11},{12,13},{... | collective-permute-start | bytes 512 | tf_op jit(solution)/shard_map/ppermute | solution.py:18
  24.4 1.3 collective-permute-start.7
  25.7 4.5 %reshape.400 = f32[16,128,308]{2,1,0:T(8,128)} reshape(f32[16,39424]{1,0:T(8,128)S(1)} %convolution_bitcast_fusion) | data formatting | bytes 5046272 | tf_op jit(solution)/shard_map/reshape | solution.py:93
  30.2 2.4 copy.25
  33.3 25.4 %all-gather.4.cloned.1.call-done = bf16[1024,3072]{1,0:T(8,128)(2,1)} async-done(((bf16[256,3072]{1,0:T(8,128)(2,1)}), bf16[1024,3072]{1,0:T(8,128)(2,1)}) %all-gather.4.cloned.1.call-update) | async-done | bytes 6291472 | tf_op jit(solution)/shard_map/all_gather | solution.py:75
  58.7 3.9 %convolution_convert_fusion.1 = bf16[128,3072]{1,0:T(8,128)(2,1)S(1)} fusion(bf16[128,1024]{1,0:T(8,128)(2,1)} %bitcast.59, bf16[1024,3072]{1,0:T(8,128)(2,1)} %all-gather.4.cloned.1.call-done), kind=kOutput, calls=%fused_computation.9 | convolution fusion | flops 805699584 | bytes 7340032 | tf_op jit(solution)/shard_map/dot_general | solution.py:82
  62.7 1.3 collective-permute-start.1
  64.0 3.0 collective-permute-start
  68.1 1.0 pad_maximum_fusion.3
  69.2 4.1 %collective-permute-start.2 = (bf16[14,3,2048]{2,1,0:T(4,128)(2,1)}, bf16[14,3,2048]{2,1,0:T(4,128)(2,1)}, u32[]{:S(2)}, u32[]{:S(2)}) collective-permute-start(bf16[14,3,2048]{2,1,0:T(4,128)(2,1)} %get-tuple-element.60), channel_id=1, source_target_pairs={{0,1},{1,2},{2,3},{4,5},{5,6},{6,7},{8,9},{9,10},{10,11},{12,13},{... | collective-permute-start | bytes 516104 | tf_op jit(solution)/shard_map/ppermute | solution.py:18
  73.3 1.5 collective-permute-start.3
  74.8 8.1 %all-gather.6.cloned.1.call-done = bf16[1024,1024]{1,0:T(8,128)(2,1)} async-done(((bf16[256,1024]{1,0:T(8,128)(2,1)}), bf16[1024,1024]{1,0:T(8,128)(2,1)}) %all-gather.6.cloned.1.call-update) | async-done | bytes 2097168 | tf_op jit(solution)/shard_map/all_gather | solution.py:76
  82.9 3.2 convolution_convert_fusion.4
  86.1 1.8 copy.26
  88.7 1.8 copy.24
  90.5 3.1 pad_maximum_fusion
  93.5 2.4 reshape.397
  95.9 2.4 fusion.60
  98.3 1.4 copy.34
  99.8 2.2 copy.35
  102.0 1.8 fusion.65
  105.0 1.8 multiply_reduce_fusion
  106.8 2.4 convolution_bitcast_fusion.1
  109.2 0.9 subtract_multiply_fusion
  110.1 3.2 copy.30
  113.3 3.0 reshape.405
  116.3 3.1 multiply_bitcast_fusion
  119.3 3.2 copy.29
  122.5 3.0 reshape.404
  125.5 1.5 constant_dynamic-update-slice_fusion.1
  127.4 1.6 copy-done.3
  129.0 1.1 fusion.59
  130.1 3.0 collective-permute-start.8
  133.7 1.5 collective-permute-start.9
  135.2 1.5 fusion.11
  136.7 2.3 copy.32
  139.0 1.5 slice.206
  140.5 5.4 %dot_general.55 = f32[4,4,39424]{2,1,0:T(4,128)} reshape(f32[16,128,308]{2,1,0:T(8,128)} %copy.32) | data formatting | bytes 5046272 | tf_op jit(solution)/shard_map/dot_general | solution.py:120
  145.9 1.3 fusion.38
  147.2 1.4 fusion.37
  149.5 4.1 %collective-permute-start.10 = (bf16[8,3,2048]{2,1,0:T(4,128)(2,1)S(1)}, bf16[8,3,2048]{2,1,0:T(4,128)(2,1)}, u32[]{:S(2)}, u32[]{:S(2)}) collective-permute-start(bf16[8,3,2048]{2,1,0:T(4,128)(2,1)S(1)} %get-tuple-element.63), channel_id=1, source_target_pairs={{0,1},{1,2},{2,3},{4,5},{5,6},{6,7},{8,9},{9,10},{10,11},{12,13},{... | collective-permute-start | bytes 294920 | tf_op jit(solution)/shard_map/ppermute | solution.py:27
  153.5 3.4 fusion.12
  157.6 1.1 concatenate.46
  159.5 1.3 collective-permute-start.11
  160.8 1.0 slice_add_fusion.3
  162.6 4.3 %collective-permute-done.11 = bf16[8,3,2048]{2,1,0:T(4,128)(2,1)S(1)} collective-permute-done((bf16[8,3,2048]{2,1,0:T(4,128)(2,1)}, bf16[8,3,2048]{2,1,0:T(4,128)(2,1)S(1)}, u32[]{:S(2)}, u32[]{:S(2)}) %collective-permute-start.11) | collective-permute-done | bytes 98336 | tf_op jit(solution)/shard_map/ppermute | solution.py:27
  167.8 5.2 %fusion.44 = (bf16[1024]{0:T(1024)(128)(2,1)S(1)}, f32[8,16]{1,0:T(8,128)S(1)}, f32[8,16]{1,0:T(8,128)S(1)}, f32[8,16,1024]{2,1,0:T(8,128)S(1)}) fusion(bf16[8,16,1024]{2,1,0:T(8,128)(2,1)S(1)} %copy-done.8, f32[8,16]{1,0:T(8,128)S(1)} %copy-done.19, f32[8,16]{1,0:T(8,128)S(1)} %broadcast_multiply_fusion.2, f32[1024]{0:T(1024)S(1)} %copy-done.22, ...), kind=kOutput, calls=%fused_computation.61 | convolution fusion | flops 808057600 | bytes 7872512 | tf_op jit(solution)/shard_map/dot_general | solution.py:156
  173.3 4.7 %convolution_convert_fusion = bf16[1024,3200]{1,0:T(8,128)(2,1)} fusion(bf16[128,1024]{1,0:T(8,128)(2,1)S(1)} %bitcast.60, bf16[128,2048]{1,0:T(8,128)(2,1)S(1)} %bitcast.67, bf16[128,1024]{1,0:T(8,128)(2,1)S(1)} %copy.31), kind=kOutput, calls=%fused_computation.4 | convolution fusion | flops 845004800 | bytes 7602176 | tf_op jit(solution)/shard_map/dot_general | solution.py:175
  178.0 0.9 maximum_dynamic-update-slice_fusion
  179.9 2.0 convolution_convert_fusion.2
  182.0 58.7 %reduce-scatter.5.cloned.1.call-done = bf16[256,3200]{1,0:T(8,128)(2,1)} async-done(((bf16[1024,3200]{1,0:T(8,128)(2,1)}), bf16[256,3200]{1,0:T(8,128)(2,1)}) %reduce-scatter.5.cloned.1.call-update) | async-done | bytes 1638416 | tf_op jit(solution)/shard_map/reduce_scatter | solution.py:180
  240.7 34.5 %reduce-scatter.9.cloned.1.call-done = bf16[256,1024]{1,0:T(8,128)(2,1)} async-done(((bf16[1024,1024]{1,0:T(8,128)(2,1)}), bf16[256,1024]{1,0:T(8,128)(2,1)}) %reduce-scatter.9.cloned.1.call-update) | async-done | bytes 524304 | tf_op jit(solution)/shard_map/reduce_scatter | solution.py:109
  275.3 38.4 %reduce-scatter.7.cloned.1.call-done = bf16[64,3200]{1,0:T(8,128)(2,1)} async-done(((bf16[256,3200]{1,0:T(8,128)(2,1)}), bf16[64,3200]{1,0:T(8,128)(2,1)}) %reduce-scatter.7.cloned.1.call-update) | async-done | bytes 409616 | tf_op jit(solution)/shard_map/reduce_scatter | solution.py:31
  313.8 1.1 fusion.43
  314.8 21.8 %reduce-scatter.11.cloned.1.call-done = bf16[64,1024]{1,0:T(8,128)(2,1)} async-done(((bf16[256,1024]{1,0:T(8,128)(2,1)}), bf16[64,1024]{1,0:T(8,128)(2,1)}) %reduce-scatter.11.cloned.1.call-update) | async-done | bytes 131088 | tf_op jit(solution)/shard_map/reduce_scatter | solution.py:31
  336.7 18.6 %all_gather.15 = bf16[256,1024]{1,0:T(8,128)(2,1)S(1)} all-gather(bf16[64,1024]{1,0:T(8,128)(2,1)} %reduce-scatter.11.cloned.1.call-done), channel_id=1, replica_groups=mesh['grp'=2,'row'=4,'col'=4] {'col'}, dimensions={0}, use_global_device_ids=true | all-gather | bytes 655360 | tf_op jit(solution)/shard_map/all_gather | solution.py:32
  355.3 1.1 convert_element_type.74
  356.4 19.8 %all-gather.8.cloned.1.call-done = bf16[256,3200]{1,0:T(8,128)(2,1)} async-done(((bf16[64,3200]{1,0:T(8,128)(2,1)}), bf16[256,3200]{1,0:T(8,128)(2,1)}) %all-gather.8.cloned.1.call-update) | async-done | bytes 1638416 | tf_op jit(solution)/shard_map/all_gather | solution.py:32
  376.2 1.8 convert_element_type.72
  379.3 2.0 slice.216
  (123 shorter events, 16.5 us)
Async XLA Ops:
  7.2 8.4 %copy-start = (f32[16,49]{1,0:T(8,128)S(1)}, f32[16,49]{1,0:T(8,128)}, u32[]{:S(2)}) copy-start(f32[16,49]{1,0:T(8,128)} %param.20) | copy-start | bytes 9412
  7.2 7.1 %copy-start.7 = (bf16[8,16,1024]{2,1,0:T(8,128)(2,1)S(1)}, bf16[8,16,1024]{2,1,0:T(8,128)(2,1)}, u32[]{:S(2)}) copy-start(bf16[8,16,1024]{2,1,0:T(8,128)(2,1)} %param.15) | copy-start | bytes 786436
  7.2 7.4 %copy-start.21 = (f32[1024]{0:T(1024)S(1)}, f32[1024]{0:T(1024)}, u32[]{:S(2)}) copy-start(f32[1024]{0:T(1024)} %param.19) | copy-start | bytes 12292
  7.2 51.5 %all-gather.4.cloned.1.call-start = ((), (), s32[]{:S(2)}) async-start(), calls=%async_computation.4 | async-start | bytes 7864320 | tf_op jit(solution)/shard_map/all_gather | solution.py:75
  7.9 75.0 %all-gather.6.cloned.1.call-start = ((), (), s32[]{:S(2)}) async-start(), calls=%async_computation.5 | async-start | bytes 2621440 | tf_op jit(solution)/shard_map/all_gather | solution.py:76
  8.8 11.3 %collective-permute-start.4 = (s32[3,16]{1,0:T(4,128)S(1)}, s32[3,16]{1,0:T(4,128)S(1)}, u32[]{:S(2)}, u32[]{:S(2)}) collective-permute-start(s32[3,16]{1,0:T(4,128)S(1)} %get-tuple-element.68), channel_id=1, source_target_pairs={{0,4},{4,8},{8,12},{1,5},{5,9},{9,13},{2,6},{6,10},{10,14},{3,7},{... | collective-permute-start | bytes 584 | tf_op jit(solution)/shard_map/ppermute | solution.py:18
  11.1 8.9 %collective-permute-start.5 = (s32[3,16]{1,0:T(4,128)S(1)}, s32[3,16]{1,0:T(4,128)S(1)}, u32[]{:S(2)}, u32[]{:S(2)}) collective-permute-start(s32[3,16]{1,0:T(4,128)S(1)} %get-tuple-element.69), channel_id=1, source_target_pairs={{4,0},{8,4},{12,8},{5,1},{9,5},{13,9},{6,2},{10,6},{14,10},{7,3},{... | collective-permute-start | bytes 584 | tf_op jit(solution)/shard_map/ppermute | solution.py:19
  12.4 228.2 %reduce-scatter.5.cloned.1.call-start = ((), (), s32[]{:S(2)}) async-start(), calls=%async_computation.6 | async-start | bytes 8192000 | tf_op jit(solution)/shard_map/reduce_scatter | solution.py:180
  14.6 5.4 %copy-start.20 = (s32[8,16]{1,0:T(8,128)S(1)}, s32[8,16]{1,0:T(8,128)}, u32[]{:S(2)}) copy-start(s32[8,16]{1,0:T(8,128)} %param.21) | copy-start | bytes 1540
  14.6 5.5 %copy-start.18 = (f32[8,16]{1,0:T(8,128)}, f32[8,16]{1,0:T(8,128)S(1)}, u32[]{:S(2)}) copy-start(f32[8,16]{1,0:T(8,128)S(1)} %add_rsqrt_fusion) | copy-start | bytes 1540
  20.1 12.5 %collective-permute-start.6 = (s32[14,3]{1,0:T(8,128)S(1)}, s32[14,3]{1,0:T(8,128)S(1)}, u32[]{:S(2)}, u32[]{:S(2)}) collective-permute-start(s32[14,3]{1,0:T(8,128)S(1)} %get-tuple-element.66), channel_id=1, source_target_pairs={{0,1},{1,2},{2,3},{4,5},{5,6},{6,7},{8,9},{9,10},{10,11},{12,13},{... | collective-permute-start | bytes 512 | tf_op jit(solution)/shard_map/ppermute | solution.py:18
  24.4 8.2 %collective-permute-start.7 = (s32[14,3]{1,0:T(8,128)S(1)}, s32[14,3]{1,0:T(8,128)S(1)}, u32[]{:S(2)}, u32[]{:S(2)}) collective-permute-start(s32[14,3]{1,0:T(8,128)S(1)} %get-tuple-element.67), channel_id=1, source_target_pairs={{1,0},{2,1},{3,2},{5,4},{6,5},{7,6},{9,8},{10,9},{11,10},{13,12},{... | collective-permute-start | bytes 512 | tf_op jit(solution)/shard_map/ppermute | solution.py:19
  58.7 8.3 %copy-start.23 = (s32[308]{0:T(512)S(1)}, s32[308]{0:T(512)}, u32[]{:S(2)}) copy-start(s32[308]{0:T(512)} %iota.114) | copy-start | bytes 3700
  58.7 8.3 %copy-start.24 = (s32[308]{0:T(512)S(1)}, s32[308]{0:T(512)}, u32[]{:S(2)}) copy-start(s32[308]{0:T(512)} %iota.108) | copy-start | bytes 3700
  58.7 8.4 %copy-start.25 = (s32[128]{0:T(128)S(1)}, s32[128]{0:T(128)}, u32[]{:S(2)}) copy-start(s32[128]{0:T(128)} %iota.117) | copy-start | bytes 1540
  58.7 8.4 %copy-start.26 = (s32[128]{0:T(128)S(1)}, s32[128]{0:T(128)}, u32[]{:S(2)}) copy-start(s32[128]{0:T(128)} %iota.111) | copy-start | bytes 1540
  58.7 8.4 %copy-start.27 = (pred[308]{0:T(512)(128)(4,1)S(1)}, pred[308]{0:T(512)(128)(4,1)}, u32[]{:S(2)}) copy-start(pred[308]{0:T(512)(128)(4,1)} %eq.44) | copy-start | bytes 928
  62.7 4.7 %collective-permute-start.1 = (bf16[3,16,2048]{2,1,0:T(8,128)(2,1)S(1)}, bf16[3,16,2048]{2,1,0:T(8,128)(2,1)S(1)}, u32[]{:S(2)}, u32[]{:S(2)}) collective-permute-start(bf16[3,16,2048]{2,1,0:T(8,128)(2,1)S(1)} %bitcast.75), channel_id=1, source_target_pairs={{4,0},{8,4},{12,8},{5,1},{9,5},{13,9},{6,2},{10,6},{14,10},{7,3},{... | collective-permute-start | bytes 589832 | tf_op jit(solution)/shard_map/ppermute | solution.py:19
  64.0 4.1 %collective-permute-start = (bf16[3,16,2048]{2,1,0:T(8,128)(2,1)S(1)}, bf16[3,16,2048]{2,1,0:T(8,128)(2,1)S(1)}, u32[]{:S(2)}, u32[]{:S(2)}) collective-permute-start(bf16[3,16,2048]{2,1,0:T(8,128)(2,1)S(1)} %bitcast.74), channel_id=1, source_target_pairs={{0,4},{4,8},{8,12},{1,5},{5,9},{9,13},{2,6},{6,10},{10,14},{3,7},{... | collective-permute-start | bytes 589832 | tf_op jit(solution)/shard_map/ppermute | solution.py:18
  67.3 0.8 copy-start.5
  67.4 1.8 copy-start.14
  68.1 1.1 copy-start.15
  69.2 21.3 %collective-permute-start.2 = (bf16[14,3,2048]{2,1,0:T(4,128)(2,1)}, bf16[14,3,2048]{2,1,0:T(4,128)(2,1)}, u32[]{:S(2)}, u32[]{:S(2)}) collective-permute-start(bf16[14,3,2048]{2,1,0:T(4,128)(2,1)} %get-tuple-element.60), channel_id=1, source_target_pairs={{0,1},{1,2},{2,3},{4,5},{5,6},{6,7},{8,9},{9,10},{10,11},{12,13},{... | collective-permute-start | bytes 516104 | tf_op jit(solution)/shard_map/ppermute | solution.py:18
  73.3 17.1 %collective-permute-start.3 = (bf16[14,3,2048]{2,1,0:T(4,128)(2,1)}, bf16[14,3,2048]{2,1,0:T(4,128)(2,1)}, u32[]{:S(2)}, u32[]{:S(2)}) collective-permute-start(bf16[14,3,2048]{2,1,0:T(4,128)(2,1)} %get-tuple-element.61), channel_id=1, source_target_pairs={{1,0},{2,1},{3,2},{5,4},{6,5},{7,6},{9,8},{10,9},{11,10},{13,12},{... | collective-permute-start | bytes 516104 | tf_op jit(solution)/shard_map/ppermute | solution.py:19
  103.9 1.1 copy-start.13
  103.9 1.2 copy-start.17
  125.5 1.8 copy-start.4
  127.4 1.6 copy-start.3
  130.1 15.7 %collective-permute-start.8 = (f32[3,22,2048]{2,1,0:T(8,128)}, f32[3,22,2048]{2,1,0:T(8,128)}, u32[]{:S(2)}, u32[]{:S(2)}) collective-permute-start(f32[3,22,2048]{2,1,0:T(8,128)} %get-tuple-element.57), channel_id=1, source_target_pairs={{0,4},{4,8},{8,12},{1,5},{5,9},{9,13},{2,6},{6,10},{10,14},{3,7},{... | collective-permute-start | bytes 1622024 | tf_op jit(solution)/shard_map/ppermute | solution.py:27
  133.7 13.5 %collective-permute-start.9 = (f32[3,22,2048]{2,1,0:T(8,128)}, f32[3,22,2048]{2,1,0:T(8,128)}, u32[]{:S(2)}, u32[]{:S(2)}) collective-permute-start(f32[3,22,2048]{2,1,0:T(8,128)} %get-tuple-element.56), channel_id=1, source_target_pairs={{4,0},{8,4},{12,8},{5,1},{9,5},{13,9},{6,2},{10,6},{14,10},{7,3},{... | collective-permute-start | bytes 1622024 | tf_op jit(solution)/shard_map/ppermute | solution.py:27
  147.2 6.4 %copy-start.9 = (f32[4,4,39424]{2,1,0:T(4,128)S(1)}, f32[4,4,39424]{2,1,0:T(4,128)}, u32[]{:S(2)}) copy-start(f32[4,4,39424]{2,1,0:T(4,128)} %dot_general.55) | copy-start | bytes 7569412
  148.5 8.4 %copy-start.11 = (bf16[16,64,128]{2,1,0:T(8,128)(2,1)S(1)}, bf16[16,64,128]{2,1,0:T(8,128)(2,1)}, u32[]{:S(2)}) copy-start(bf16[16,64,128]{2,1,0:T(8,128)(2,1)} %fusion.11) | copy-start | bytes 786436
  149.5 11.3 %collective-permute-start.10 = (bf16[8,3,2048]{2,1,0:T(4,128)(2,1)S(1)}, bf16[8,3,2048]{2,1,0:T(4,128)(2,1)}, u32[]{:S(2)}, u32[]{:S(2)}) collective-permute-start(bf16[8,3,2048]{2,1,0:T(4,128)(2,1)S(1)} %get-tuple-element.63), channel_id=1, source_target_pairs={{0,1},{1,2},{2,3},{4,5},{5,6},{6,7},{8,9},{9,10},{10,11},{12,13},{... | collective-permute-start | bytes 294920 | tf_op jit(solution)/shard_map/ppermute | solution.py:27
  159.4 8.4 %copy-start.8 = (bf16[8,16,1024]{2,1,0:T(8,128)(2,1)S(1)}, bf16[8,16,1024]{2,1,0:T(8,128)(2,1)}, u32[]{:S(2)}) copy-start(bf16[8,16,1024]{2,1,0:T(8,128)(2,1)} %param.15) | copy-start | bytes 786436
  159.4 8.4 %copy-start.19 = (f32[8,16]{1,0:T(8,128)S(1)}, f32[8,16]{1,0:T(8,128)}, u32[]{:S(2)}) copy-start(f32[8,16]{1,0:T(8,128)} %copy-done.18) | copy-start | bytes 1540
  159.4 8.4 %copy-start.22 = (f32[1024]{0:T(1024)S(1)}, f32[1024]{0:T(1024)}, u32[]{:S(2)}) copy-start(f32[1024]{0:T(1024)} %param.19) | copy-start | bytes 12292
  159.5 7.4 %collective-permute-start.11 = (bf16[8,3,2048]{2,1,0:T(4,128)(2,1)}, bf16[8,3,2048]{2,1,0:T(4,128)(2,1)S(1)}, u32[]{:S(2)}, u32[]{:S(2)}) collective-permute-start(bf16[8,3,2048]{2,1,0:T(4,128)(2,1)} %get-tuple-element.62), channel_id=1, source_target_pairs={{1,0},{2,1},{3,2},{5,4},{6,5},{7,6},{9,8},{10,9},{11,10},{13,12},{... | collective-permute-start | bytes 294920 | tf_op jit(solution)/shard_map/ppermute | solution.py:27
  167.8 5.5 %copy-start.6 = (bf16[8,16,1024]{2,1,0:T(8,128)(2,1)S(1)}, bf16[8,16,1024]{2,1,0:T(8,128)(2,1)}, u32[]{:S(2)}) copy-start(bf16[8,16,1024]{2,1,0:T(8,128)(2,1)} %fusion.39) | copy-start | bytes 786436
  173.3 4.7 %copy-start.12 = (bf16[4,256,49]{2,1,0:T(8,128)(2,1)S(1)}, bf16[4,256,49]{2,1,0:T(8,128)(2,1)}, u32[]{:S(2)}) copy-start(bf16[4,256,49]{2,1,0:T(8,128)(2,1)} %pad.18) | copy-start | bytes 301060
  173.3 4.7 %copy-start.28 = (bf16[128]{0:T(256)(128)(2,1)S(1)}, bf16[128]{0:T(256)(128)(2,1)}, u32[]{:S(2)}) copy-start(bf16[128]{0:T(256)(128)(2,1)} %pad.21.clone) | copy-start | bytes 772
  178.9 0.9 copy-start.10
  178.9 1.0 copy-start.16
  178.9 96.3 %reduce-scatter.9.cloned.1.call-start = ((), (), s32[]{:S(2)}) async-start(), calls=%async_computation.9 | async-start | bytes 2621440 | tf_op jit(solution)/shard_map/reduce_scatter | solution.py:109
  181.9 131.8 %reduce-scatter.7.cloned.1.call-start = ((), (), s32[]{:S(2)}) async-start(), calls=%async_computation.7 | async-start | bytes 2048000 | tf_op jit(solution)/shard_map/reduce_scatter | solution.py:31
  240.7 96.0 %reduce-scatter.11.cloned.1.call-start = ((), (), s32[]{:S(2)}) async-start(), calls=%async_computation.10 | async-start | bytes 655360 | tf_op jit(solution)/shard_map/reduce_scatter | solution.py:31
  275.3 100.9 %all-gather.8.cloned.1.call-start = ((), (), s32[]{:S(2)}) async-start(), calls=%async_computation.8 | async-start | bytes 2048000 | tf_op jit(solution)/shard_map/all_gather | solution.py:32
  376.2 2.5 copy-start.2
  378.7 2.7 copy-start.1
Sparse Core Ops, SparseCore 0:
  9.6 49.0 all-gather.3
  60.3 22.5 all-gather.5
  179.0 61.5 reduce-scatter.4
  243.8 31.4 reduce-scatter.8
  277.4 36.2 reduce-scatter.6
  316.0 20.6 reduce-scatter.10
  338.3 37.8 all-gather.7

commit v3 on v1

--- a/solution.py
+++ b/solution.py
@@ -76,15 +76,16 @@
     flat = normed_features.reshape(-1, width)
     joined = jnp.dot(flat, full_qkv, preferred_element_type=jnp.float32).astype(jnp.bfloat16)
     query = joined[:, :width]
-    kv = joined[:, width:].reshape(rows, cols, 2 * width)
-    kv_ext = extended_2(kv, (("row", 0), ("col", 1)), reach).reshape(nk, 2 * width)
-    mask_ext = extended_2(valid_mask, (("row", 0), ("col", 1)), reach).reshape(nk)
+    flags = jnp.broadcast_to(valid_mask.astype(jnp.bfloat16)[:, :, None], (rows, cols, 128))
+    kv = jnp.concatenate([joined[:, width:].reshape(rows, cols, 2 * width), flags], axis=-1)
+    kv_ext = extended_2(kv, (("row", 0), ("col", 1)), reach).reshape(nk, 2 * width + 128)
+    mask_ext = kv_ext[:, 2 * width]
     q3 = query.reshape(nq, heads, hdim)
     k3 = kv_ext[:, :width].reshape(nk, heads, hdim)
-    v3 = kv_ext[:, width:].reshape(nk, heads, hdim)
+    v3 = kv_ext[:, width : 2 * width].reshape(nk, heads, hdim)
 
     inside, centre, one_hot = window_tables(rows, cols, reach)
-    allowed = inside & ((mask_ext[None, :] == 1) | centre)
+    allowed = inside & ((mask_ext[None, :] == 1.0) | centre)
     bias_full = jnp.dot(pos_bias, one_hot, precision=HIGHEST).reshape(heads, nq, nk)
     raw = jnp.einsum("phd,khd->hpk", q3, k3, preferred_element_type=jnp.float32)
     scores = jnp.where(allowed[None], raw * scale + bias_full, -jnp.inf)

time: 350 us -> 353 us (level)
  waiting for transfers between devices: 192 us -> 206 us
  starting transfers between devices: 28.8 us -> 18.6 us
  local copies, waits for them, and re-layouts: 63.6 us -> 59.9 us
    all_gather x1, waiting for transfers between devices: 25.4 us -> 46.1 us  [body(): lax.all_gather(qkv_weight, 'row', axis=0, tiled=True)]
    all_gather x1, waiting for transfers between devices: 8.16 us -> 0.02 us  [body(): lax.all_gather(out_weight, 'row', axis=0, tiled=True)]
    ppermute x4 -> x2, starting transfers between devices: 13.8 us -> 6.95 us  [extended_2(): before = lax.ppermute(last, axis, up)]
    unnamed x65 -> x51, local copies, waits for them, and re-layouts: 8.82 us -> 5.07 us
    reduce_scatter x1, waiting for transfers between devices: 62 us -> 58.5 us  [body(): lax.psum_scatter(big, 'row', scatter_dimension=0, tiled=True)]
  transfers between devices with their start and end apart: 17 -> 13, of which waited for: 6 -> 5; matrix products, arithmetic and copies ran while one was open for 19% -> 18% of each run, Pallas kernels for 0% -> 0%
where the time goes in v3:
time: 353 us; the launch traced here: 352 us
  waiting for transfers between devices  206 us (58%)
  local copies, waits for them, and re-layouts  59.9 us (17%)
  matrix products  37 us (10%)
  starting transfers between devices  18.6 us (5%)
  other arithmetic  16.2 us (5%)
  between operations  14.3 us (4%)
    psum x1, waiting for transfers between devices, body(): lax.psum(lax.psum_scatter(big, 'row', scatter_dimension=0, tiled=True), '...  90.8 us
    reduce_scatter x1, waiting for transfers between devices, body(): lax.psum_scatter(big, 'row', scatter_dimension=0, tiled=True)  58.5 us
    all_gather x1, waiting for transfers between devices, body(): lax.all_gather(qkv_weight, 'row', axis=0, tiled=True)  46.1 us
    ppermute x4, starting transfers between devices, passed_along(): lax.ppermute(value, axis, [(source, source + steps) for source in range(f...  8.75 us
  transfers between devices with their start and end apart: 13, of which 5 were waited for; matrix products, arithmetic and copies ran while one was open for 18% of the time, Pallas kernels for 0%

profile of v3, /device:TPU:0, one launch (start us, length us, event | category | flops | bytes accessed | tf_op | source)
XLA Modules:
  0.0 351.6 jit_solution(638585926524188837)
XLA Ops:
  8.0 0.7 all-gather.5.cloned.1.call-update
  12.6 46.1 %all-gather.3.cloned.1.call-done = bf16[1024,3072]{1,0:T(8,128)(2,1)} async-done(((bf16[256,3072]{1,0:T(8,128)(2,1)}), bf16[1024,3072]{1,0:T(8,128)(2,1)}) %all-gather.3.cloned.1.call-update) | async-done | bytes 6291472 | tf_op jit(solution)/shard_map/all_gather | solution.py:70
  58.7 3.8 %convolution_convert_fusion.1 = bf16[128,3072]{1,0:T(8,128)(2,1)S(1)} fusion(bf16[128,1024]{1,0:T(8,128)(2,1)S(1)} %bitcast.58, bf16[1024,3072]{1,0:T(8,128)(2,1)} %all-gather.3.cloned.1.call-done), kind=kOutput, calls=%fused_computation.9 | convolution fusion | flops 805699584 | bytes 7340032 | tf_op jit(solution)/shard_map/dot_general | solution.py:77
  62.7 0.9 pad_maximum_fusion.6
  63.5 2.8 collective-permute-start
  66.4 1.3 collective-permute-start.1
  67.7 3.1 convolution_bitcast_fusion
  70.8 4.5 %reshape.399 = f32[16,128,308]{2,1,0:T(8,128)} reshape(f32[16,39424]{1,0:T(8,128)S(1)} %convolution_bitcast_fusion) | data formatting | bytes 5046272 | tf_op jit(solution)/shard_map/reshape | solution.py:89
  75.3 2.4 copy.35
  77.7 2.1 pad_maximum_fusion.4
  79.8 4.1 %collective-permute-start.2 = (bf16[14,3,2176]{2,1,0:T(4,128)(2,1)}, bf16[14,3,2176]{2,1,0:T(4,128)(2,1)}, u32[]{:S(2)}, u32[]{:S(2)}) collective-permute-start(bf16[14,3,2176]{2,1,0:T(4,128)(2,1)} %get-tuple-element.62), channel_id=1, source_target_pairs={{0,1},{1,2},{2,3},{4,5},{5,6},{6,7},{8,9},{9,10},{10,11},{12,13},{... | collective-permute-start | bytes 548360 | tf_op jit(solution)/shard_map/ppermute | solution.py:18
  83.9 1.5 collective-permute-start.3
  85.4 3.2 convolution_convert_fusion.4
  88.6 1.8 copy.36
  90.4 0.8 copy.34
  91.2 3.5 collective-permute-done.3
  94.7 3.0 pad_maximum_fusion
  97.7 2.4 reshape.396
  100.2 1.0 compare_reduce_fusion
  101.2 2.4 fusion.60
  103.6 1.4 copy.33
  105.1 2.2 copy.37
  107.5 1.8 fusion.62
  109.8 0.8 copy-done.15
  110.6 1.8 multiply_reduce_fusion
  112.4 2.4 convolution_bitcast_fusion.1
  114.8 0.9 subtract_multiply_fusion
  115.6 3.2 copy.40
  118.8 3.0 reshape.404
  121.9 3.1 multiply_bitcast_fusion
  125.0 3.2 copy.39
  128.1 3.0 reshape.403
  131.1 1.5 constant_dynamic-update-slice_fusion.1
  133.0 1.6 copy-done.3
  134.6 1.1 fusion.59
  135.7 2.7 collective-permute-start.4
  138.5 2.1 convolution_convert_fusion.2
  141.3 1.5 collective-permute-start.5
  142.8 1.5 fusion.11
  144.2 2.3 copy.42
  146.6 1.8 slice.181
  148.3 5.4 %dot_general.55 = f32[4,4,39424]{2,1,0:T(4,128)} reshape(f32[16,128,308]{2,1,0:T(8,128)} %copy.42) | data formatting | bytes 5046272 | tf_op jit(solution)/shard_map/dot_general | solution.py:116
  153.8 1.3 fusion.38
  155.1 1.4 fusion.37
  156.6 0.8 fusion.61
  157.4 3.2 collective-permute-start.6
  160.7 3.4 fusion.12
  164.7 1.1 concatenate.42
  165.8 0.7 pad.18
  166.6 1.3 collective-permute-start.7
  167.9 1.0 slice_add_fusion.3
  168.9 0.8 scatter-add.16
  169.7 5.3 %collective-permute-done.7 = bf16[8,3,2048]{2,1,0:T(4,128)(2,1)S(1)} collective-permute-done((bf16[8,3,2048]{2,1,0:T(4,128)(2,1)}, bf16[8,3,2048]{2,1,0:T(4,128)(2,1)S(1)}, u32[]{:S(2)}, u32[]{:S(2)}) %collective-permute-start.7) | collective-permute-done | bytes 98336 | tf_op jit(solution)/shard_map/ppermute | solution.py:27
  175.1 0.7 scatter-add.19
  175.9 5.3 %fusion.44 = (bf16[1024]{0:T(1024)(128)(2,1)S(1)}, f32[8,16]{1,0:T(8,128)S(1)}, f32[8,16]{1,0:T(8,128)S(1)}, f32[8,16,1024]{2,1,0:T(8,128)S(1)}) fusion(bf16[8,16,1024]{2,1,0:T(8,128)(2,1)S(1)} %copy-done.8, f32[8,16]{1,0:T(8,128)S(1)} %add_rsqrt_fusion, f32[8,16]{1,0:T(8,128)S(1)} %broadcast_multiply_fusion.2, f32[1024]{0:T(1024)S(1)} %copy-done.20, ...), kind=kOutput, calls=%fused_computation.61 | convolution fusion | flops 808057600 | bytes 7872512 | tf_op jit(solution)/shard_map/dot_general | solution.py:152
  181.4 4.6 %convolution_convert_fusion = bf16[1024,3200]{1,0:T(8,128)(2,1)} fusion(bf16[128,1024]{1,0:T(8,128)(2,1)S(1)} %bitcast.59, bf16[128,2048]{1,0:T(8,128)(2,1)S(1)} %bitcast.66, bf16[128,1024]{1,0:T(8,128)(2,1)S(1)} %copy.41), kind=kOutput, calls=%fused_computation.4 | convolution fusion | flops 845004800 | bytes 7602176 | tf_op jit(solution)/shard_map/dot_general | solution.py:171
  186.0 0.9 maximum_dynamic-update-slice_fusion
  187.0 58.5 %reduce-scatter.3.cloned.1.call-done = bf16[256,3200]{1,0:T(8,128)(2,1)} async-done(((bf16[1024,3200]{1,0:T(8,128)(2,1)}), bf16[256,3200]{1,0:T(8,128)(2,1)}) %reduce-scatter.3.cloned.1.call-update) | async-done | bytes 1638416 | tf_op jit(solution)/shard_map/reduce_scatter | solution.py:176
  245.6 1.1 fusion.43
  246.6 90.8 %all-reduce.5.cloned.1.call-done = (bf16[256,3200]{1,0:T(8,128)(2,1)}, bf16[256,1024]{1,0:T(8,128)(2,1)}) async-done(((bf16[256,3200]{1,0:T(8,128)(2,1)}, bf16[256,1024]{1,0:T(8,128)(2,1)}), (bf16[256,3200]{1,0:T(8,128)(2,1)}, bf16[256,1024]{1,0:T(8,128)(2,1)})) %all-reduce.5.cloned.1.call-update) | async-done | bytes 2162704 | tf_op jit(solution)/shard_map/psum | solution.py:176
  337.4 1.3 slice.193
  338.7 3.6 %slice.191 = f32[256,3072]{1,0:T(8,128)} slice(bf16[256,3200]{1,0:T(8,128)(2,1)} %get-tuple-element.56), slice={[0:256], [0:3072]} | slice | bytes 6291456 | tf_op jit(solution)/shard_map/slice | solution.py:178
  342.5 0.8 copy-done.16
  343.4 1.1 convert_element_type.78
  (99 shorter events, 8.6 us)
Async XLA Ops:
  7.2 60.5 %copy-start = (f32[16,49]{1,0:T(8,128)S(1)}, f32[16,49]{1,0:T(8,128)}, u32[]{:S(2)}) copy-start(f32[16,49]{1,0:T(8,128)} %param.20) | copy-start | bytes 9412
  7.2 4.9 %copy-start.7 = (bf16[8,16,1024]{2,1,0:T(8,128)(2,1)S(1)}, bf16[8,16,1024]{2,1,0:T(8,128)(2,1)}, u32[]{:S(2)}) copy-start(bf16[8,16,1024]{2,1,0:T(8,128)(2,1)} %param.15) | copy-start | bytes 786436
  7.2 5.2 %copy-start.19 = (f32[1024]{0:T(1024)S(1)}, f32[1024]{0:T(1024)}, u32[]{:S(2)}) copy-start(f32[1024]{0:T(1024)} %param.19) | copy-start | bytes 12292
  7.2 51.5 %all-gather.3.cloned.1.call-start = ((), (), s32[]{:S(2)}) async-start(), calls=%async_computation.2 | async-start | bytes 7864320 | tf_op jit(solution)/shard_map/all_gather | solution.py:70
  7.9 77.4 %all-gather.5.cloned.1.call-start = ((), (), s32[]{:S(2)}) async-start(), calls=%async_computation.3 | async-start | bytes 2621440 | tf_op jit(solution)/shard_map/all_gather | solution.py:71
  8.7 178.3 %reduce-scatter.5.cloned.1.call-start = ((), (), s32[]{:S(2)}) async-start(), calls=%async_computation.5 | async-start | bytes 2621440 | tf_op jit(solution)/shard_map/reduce_scatter | solution.py:105
  12.6 49.9 %copy-start.5 = (bf16[8,16,1024]{2,1,0:T(8,128)(2,1)}, bf16[8,16,1024]{2,1,0:T(8,128)(2,1)S(1)}, u32[]{:S(2)}) copy-start(bf16[8,16,1024]{2,1,0:T(8,128)(2,1)S(1)} %fusion.39) | copy-start | bytes 786436
  62.5 3.9 %copy-start.9 = (bf16[128,3072]{1,0:T(8,128)(2,1)}, bf16[128,3072]{1,0:T(8,128)(2,1)S(1)}, u32[]{:S(2)}) copy-start(bf16[128,3072]{1,0:T(8,128)(2,1)S(1)} %convolution_convert_fusion.1) | copy-start | bytes 2359300
  63.5 14.2 %collective-permute-start = (bf16[3,16,2176]{2,1,0:T(8,128)(2,1)}, bf16[3,16,2176]{2,1,0:T(8,128)(2,1)}, u32[]{:S(2)}, u32[]{:S(2)}) collective-permute-start(bf16[3,16,2176]{2,1,0:T(8,128)(2,1)} %get-tuple-element.66), channel_id=1, source_target_pairs={{0,4},{4,8},{8,12},{1,5},{5,9},{9,13},{2,6},{6,10},{10,14},{3,7},{... | collective-permute-start | bytes 626696 | tf_op jit(solution)/shard_map/ppermute | solution.py:18
  66.4 11.3 %collective-permute-start.1 = (bf16[3,16,2176]{2,1,0:T(8,128)(2,1)}, bf16[3,16,2176]{2,1,0:T(8,128)(2,1)}, u32[]{:S(2)}, u32[]{:S(2)}) collective-permute-start(bf16[3,16,2176]{2,1,0:T(8,128)(2,1)} %get-tuple-element.67), channel_id=1, source_target_pairs={{4,0},{8,4},{12,8},{5,1},{9,5},{13,9},{6,2},{10,6},{14,10},{7,3},{... | collective-permute-start | bytes 626696 | tf_op jit(solution)/shard_map/ppermute | solution.py:19
  77.7 12.7 %slice-start = ((bf16[128,3072]{1,0:T(8,128)(2,1)}), bf16[128,1024]{1,0:T(8,128)(2,1)S(1)}, s32[]{:S(2)}) async-start(bf16[128,3072]{1,0:T(8,128)(2,1)} %copy-done.9), calls=%async_computation.7 | async-start | bytes 524288 | tf_op jit(solution)/shard_map/slice | solution.py:78
  79.8 11.5 %collective-permute-start.2 = (bf16[14,3,2176]{2,1,0:T(4,128)(2,1)}, bf16[14,3,2176]{2,1,0:T(4,128)(2,1)}, u32[]{:S(2)}, u32[]{:S(2)}) collective-permute-start(bf16[14,3,2176]{2,1,0:T(4,128)(2,1)} %get-tuple-element.62), channel_id=1, source_target_pairs={{0,1},{1,2},{2,3},{4,5},{5,6},{6,7},{8,9},{9,10},{10,11},{12,13},{... | collective-permute-start | bytes 548360 | tf_op jit(solution)/shard_map/ppermute | solution.py:18
  83.9 10.9 %collective-permute-start.3 = (bf16[14,3,2176]{2,1,0:T(4,128)(2,1)}, bf16[14,3,2176]{2,1,0:T(4,128)(2,1)}, u32[]{:S(2)}, u32[]{:S(2)}) collective-permute-start(bf16[14,3,2176]{2,1,0:T(4,128)(2,1)} %get-tuple-element.63), channel_id=1, source_target_pairs={{1,0},{2,1},{3,2},{5,4},{6,5},{7,6},{9,8},{10,9},{11,10},{13,12},{... | collective-permute-start | bytes 548360 | tf_op jit(solution)/shard_map/ppermute | solution.py:19
  101.2 6.1 %copy-start.21 = (s32[308]{0:T(512)S(1)}, s32[308]{0:T(512)}, u32[]{:S(2)}) copy-start(s32[308]{0:T(512)} %iota.108) | copy-start | bytes 3700
  101.2 6.1 %copy-start.22 = (s32[128]{0:T(128)S(1)}, s32[128]{0:T(128)}, u32[]{:S(2)}) copy-start(s32[128]{0:T(128)} %iota.117) | copy-start | bytes 1540
  101.2 6.1 %copy-start.23 = (s32[128]{0:T(128)S(1)}, s32[128]{0:T(128)}, u32[]{:S(2)}) copy-start(s32[128]{0:T(128)} %iota.111) | copy-start | bytes 1540
  109.4 1.1 copy-start.15
  109.4 1.2 copy-start.18
  131.1 1.8 copy-start.4
  132.9 5.6 %copy-start.11 = (bf16[8,16,1024]{2,1,0:T(8,128)(2,1)S(1)}, bf16[8,16,1024]{2,1,0:T(8,128)(2,1)}, u32[]{:S(2)}) copy-start(bf16[8,16,1024]{2,1,0:T(8,128)(2,1)} %param.16) | copy-start | bytes 786436
  132.9 5.6 %copy-start.17 = (bf16[16,64,128]{2,1,0:T(8,128)(2,1)S(1)}, bf16[16,64,128]{2,1,0:T(8,128)(2,1)}, u32[]{:S(2)}) copy-start(bf16[16,64,128]{2,1,0:T(8,128)(2,1)} %get-tuple-element.71) | copy-start | bytes 786436
  133.0 1.6 copy-start.3
  135.7 18.0 %collective-permute-start.4 = (f32[3,22,2048]{2,1,0:T(8,128)}, f32[3,22,2048]{2,1,0:T(8,128)}, u32[]{:S(2)}, u32[]{:S(2)}) collective-permute-start(f32[3,22,2048]{2,1,0:T(8,128)} %get-tuple-element.59), channel_id=1, source_target_pairs={{0,4},{4,8},{8,12},{1,5},{5,9},{9,13},{2,6},{6,10},{10,14},{3,7},{... | collective-permute-start | bytes 1622024 | tf_op jit(solution)/shard_map/ppermute | solution.py:27
  140.6 104.9 %reduce-scatter.3.cloned.1.call-start = ((), (), s32[]{:S(2)}) async-start(), calls=%async_computation.4 | async-start | bytes 8192000 | tf_op jit(solution)/shard_map/reduce_scatter | solution.py:176
  141.3 13.8 %collective-permute-start.5 = (f32[3,22,2048]{2,1,0:T(8,128)}, f32[3,22,2048]{2,1,0:T(8,128)}, u32[]{:S(2)}, u32[]{:S(2)}) collective-permute-start(f32[3,22,2048]{2,1,0:T(8,128)} %get-tuple-element.58), channel_id=1, source_target_pairs={{4,0},{8,4},{12,8},{5,1},{9,5},{13,9},{6,2},{10,6},{14,10},{7,3},{... | collective-permute-start | bytes 1622024 | tf_op jit(solution)/shard_map/ppermute | solution.py:27
  155.1 5.6 %copy-start.10 = (f32[4,4,39424]{2,1,0:T(4,128)S(1)}, f32[4,4,39424]{2,1,0:T(4,128)}, u32[]{:S(2)}) copy-start(f32[4,4,39424]{2,1,0:T(4,128)} %dot_general.55) | copy-start | bytes 7569412
  156.5 7.6 %copy-start.13 = (bf16[16,64,128]{2,1,0:T(8,128)(2,1)S(1)}, bf16[16,64,128]{2,1,0:T(8,128)(2,1)}, u32[]{:S(2)}) copy-start(bf16[16,64,128]{2,1,0:T(8,128)(2,1)} %fusion.11) | copy-start | bytes 786436
  157.4 10.5 %collective-permute-start.6 = (bf16[8,3,2048]{2,1,0:T(4,128)(2,1)S(1)}, bf16[8,3,2048]{2,1,0:T(4,128)(2,1)}, u32[]{:S(2)}, u32[]{:S(2)}) collective-permute-start(bf16[8,3,2048]{2,1,0:T(4,128)(2,1)S(1)} %get-tuple-element.65), channel_id=1, source_target_pairs={{0,1},{1,2},{2,3},{4,5},{5,6},{6,7},{8,9},{9,10},{10,11},{12,13},{... | collective-permute-start | bytes 294920 | tf_op jit(solution)/shard_map/ppermute | solution.py:27
  166.5 9.4 %copy-start.8 = (bf16[8,16,1024]{2,1,0:T(8,128)(2,1)S(1)}, bf16[8,16,1024]{2,1,0:T(8,128)(2,1)}, u32[]{:S(2)}) copy-start(bf16[8,16,1024]{2,1,0:T(8,128)(2,1)} %param.15) | copy-start | bytes 786436
  166.5 9.4 %copy-start.20 = (f32[1024]{0:T(1024)S(1)}, f32[1024]{0:T(1024)}, u32[]{:S(2)}) copy-start(f32[1024]{0:T(1024)} %param.19) | copy-start | bytes 12292
  166.6 8.4 %collective-permute-start.7 = (bf16[8,3,2048]{2,1,0:T(4,128)(2,1)}, bf16[8,3,2048]{2,1,0:T(4,128)(2,1)S(1)}, u32[]{:S(2)}, u32[]{:S(2)}) collective-permute-start(bf16[8,3,2048]{2,1,0:T(4,128)(2,1)} %get-tuple-element.64), channel_id=1, source_target_pairs={{1,0},{2,1},{3,2},{5,4},{6,5},{7,6},{9,8},{10,9},{11,10},{13,12},{... | collective-permute-start | bytes 294920 | tf_op jit(solution)/shard_map/ppermute | solution.py:27
  175.9 5.5 %copy-start.6 = (bf16[8,16,1024]{2,1,0:T(8,128)(2,1)S(1)}, bf16[8,16,1024]{2,1,0:T(8,128)(2,1)}, u32[]{:S(2)}) copy-start(bf16[8,16,1024]{2,1,0:T(8,128)(2,1)} %copy-done.5) | copy-start | bytes 786436
  181.4 4.6 %copy-start.14 = (bf16[4,256,49]{2,1,0:T(8,128)(2,1)S(1)}, bf16[4,256,49]{2,1,0:T(8,128)(2,1)}, u32[]{:S(2)}) copy-start(bf16[4,256,49]{2,1,0:T(8,128)(2,1)} %pad.18) | copy-start | bytes 301060
  181.4 4.6 %copy-start.24 = (bf16[128]{0:T(256)(128)(2,1)S(1)}, bf16[128]{0:T(256)(128)(2,1)}, u32[]{:S(2)}) copy-start(bf16[128]{0:T(256)(128)(2,1)} %pad.21.clone) | copy-start | bytes 772
  186.9 58.6 %copy-start.12 = (bf16[8,16,1024]{2,1,0:T(8,128)(2,1)S(1)}, bf16[8,16,1024]{2,1,0:T(8,128)(2,1)}, u32[]{:S(2)}) copy-start(bf16[8,16,1024]{2,1,0:T(8,128)(2,1)} %param.16) | copy-start | bytes 786436
  187.0 150.4 %all-reduce.5.cloned.1.call-start = ((), (), s32[]{:S(2)}) async-start(), calls=%async_computation.6 | async-start | bytes 4325376 | tf_op jit(solution)/shard_map/psum | solution.py:176
  338.7 3.6 %copy-start.2 = (bf16[256,3200]{1,0:T(8,128)(2,1)S(1)}, bf16[256,3200]{1,0:T(8,128)(2,1)}, u32[]{:S(2)}) copy-start(bf16[256,3200]{1,0:T(8,128)(2,1)} %get-tuple-element.56) | copy-start | bytes 4915204
  338.7 6.4 %copy-start.1 = (f32[16,49]{1,0:T(8,128)S(1)}, f32[16,49]{1,0:T(8,128)}, u32[]{:S(2)}) copy-start(f32[16,49]{1,0:T(8,128)} %param.20) | copy-start | bytes 9412
  342.3 1.0 copy-start.16
Sparse Core Ops, SparseCore 0:
  9.6 49.0 all-gather.2
  60.3 24.8 all-gather.4
  140.7 29.8 reduce-scatter.4
  187.1 58.3 reduce-scatter.2
  247.8 89.5 all-reduce.4

commit v4 on v3

--- a/solution.py
+++ b/solution.py
@@ -25,6 +25,27 @@
     count = lax.axis_size(axis)
     first, last = (max(0, -steps), min(count, count - steps))
     return lax.ppermute(value, axis, [(source, source + steps) for source in range(first, last)])
+
+
+def gathered_rows(shards):
+    count = lax.axis_size("row")
+    index = lax.axis_index("row")
+    held = [(shards, index)]
+    for step in range(2, count, 2):
+        pairs = [(r, (r + step) % count) for r in range(count)]
+        held.append((lax.ppermute(shards, "row", pairs), (index - step) % count))
+    partner = [(r, r ^ 1) for r in range(count)]
+    pieces, blocks = [p for p, _ in held], [b for _, b in held]
+    swapped = lax.ppermute(tuple(pieces), "row", partner)
+    held = held + [(piece, (b ^ 1)) for piece, b in zip(swapped, blocks)]
+    outs = []
+    for leaf in range(len(shards)):
+        size = shards[leaf].shape[0]
+        full = jnp.zeros((size * count,) + shards[leaf].shape[1:], shards[leaf].dtype)
+        for piece, block in held:
+            full = lax.dynamic_update_slice_in_dim(full, piece[leaf], block * size, axis=0)
+        outs.append(full)
+    return outs
 
 
 def apply_layer_norm(values, norm_gain_value):
@@ -66,10 +87,7 @@
     ext_rows, ext_cols = rows + 2 * reach, cols + 2 * reach
     nq, nk = rows * cols, ext_rows * ext_cols
     scale = float(hdim) ** (-0.5)
-    full_qkv, full_out = (
-        lax.all_gather(qkv_weight, "row", axis=0, tiled=True),
-        lax.all_gather(out_weight, "row", axis=0, tiled=True),
-    )
+    full_qkv, full_out = gathered_rows((qkv_weight, out_weight))
     normed_features, standardized_input, inverse_deviation = apply_layer_norm(
         patches, layer_norm_gain
     )

time: 353 us -> 347 us (0.983)
  waiting for transfers between devices: 206 us -> 191 us
  starting transfers between devices: 18.6 us -> 25.1 us
  local copies, waits for them, and re-layouts: 59.9 us -> 65.2 us
  matrix products: 37 us -> 32.4 us
    all_gather x2 -> x0, waiting for transfers between devices: 46.1 us -> none  [the longest x1 46.1 us: body(): lax.all_gather(qkv_weight, 'row', axis=0, tiled=True)]
    ppermute x0 -> x6, waiting for transfers between devices: none -> 29 us  [the longest x2 29 us: gathered_rows(): held.append((lax.ppermute(shards, 'row', pairs), (index - step) % count))]
    dynamic_update_slice x0 -> x8, local copies, waits for them, and re-layouts: none -> 7.2 us  [gathered_rows(): lax.dynamic_update_slice_in_dim(full, piece[leaf], block * size, axis=0)]
    ppermute x0 -> x6, starting transfers between devices: none -> 4.12 us  [the longest x2 3.19 us: gathered_rows(): held.append((lax.ppermute(shards, 'row', pairs), (index - step) % count))]
    ppermute x2, waiting for transfers between devices: 3.52 us -> 7.09 us  [extended_2(): after = lax.ppermute(first, axis, down)]
  transfers between devices with their start and end apart: 13 -> 17, of which waited for: 5 -> 6; matrix products, arithmetic and copies ran while one was open for 18% -> 19% of each run, Pallas kernels for 0% -> 0%
where the time goes in v4:
time: 347 us; the launch traced here: 346 us
  waiting for transfers between devices  191 us (55%)
  local copies, waits for them, and re-layouts  65.2 us (19%)
  matrix products  32.4 us (9%)
  starting transfers between devices  25.1 us (7%)
  other arithmetic  17.6 us (5%)
  between operations  14.5 us (4%)
    psum x1, waiting for transfers between devices, body(): lax.psum(lax.psum_scatter(big, 'row', scatter_dimension=0, tiled=True), '...  90.9 us
    reduce_scatter x1, waiting for transfers between devices, body(): lax.psum_scatter(big, 'row', scatter_dimension=0, tiled=True)  58.7 us
    ppermute x2, waiting for transfers between devices, gathered_rows(): held.append((lax.ppermute(shards, 'row', pairs), (index - step) % count))  29 us
    ppermute x4, starting transfers between devices, passed_along(): lax.ppermute(value, axis, [(source, source + steps) for source in range(f...  12 us
    dynamic_update_slice x8, local copies, waits for them, and re-layouts, gathered_rows(): lax.dynamic_update_slice_in_dim(full, piece[leaf], block * size, axis=0)  7.2 us
    ppermute x2, waiting for transfers between devices, extended_2(): after = lax.ppermute(first, axis, down)  7.09 us
  transfers between devices with their start and end apart: 17, of which 6 were waited for; matrix products, arithmetic and copies ran while one was open for 19% of the time, Pallas kernels for 0%

profile of v4, /device:TPU:0, one launch (start us, length us, event | category | flops | bytes accessed | tf_op | source)
XLA Modules:
  0.0 345.9 jit_solution(7014564403994310402)
XLA Ops:
  7.2 3.0 collective-permute-start
  10.8 1.1 convert_reduce_fusion
  11.8 1.1 fusion.45
  13.7 3.1 convolution_bitcast_fusion
  16.8 29.0 %collective-permute-done = bf16[256,3072]{1,0:T(8,128)(2,1)} collective-permute-done((bf16[256,3072]{1,0:T(8,128)(2,1)}, bf16[256,3072]{1,0:T(8,128)(2,1)}, u32[]{:S(2)}, u32[]{:S(2)}) %collective-permute-start) | collective-permute-done | bytes 1572896 | tf_op jit(solution)/shard_map/ppermute | solution.py:36
  48.7 4.5 %reshape.399 = f32[16,128,308]{2,1,0:T(8,128)} reshape(f32[16,39424]{1,0:T(8,128)S(1)} %convolution_bitcast_fusion) | data formatting | bytes 5046272 | tf_op jit(solution)/shard_map/reshape | solution.py:107
  53.2 2.4 copy.31
  58.1 1.1 constant_dynamic-update-slice_fusion.4
  59.2 1.6 constant_dynamic-update-slice_fusion.8
  60.8 1.6 constant_dynamic-update-slice_fusion.7
  62.4 1.6 constant_dynamic-update-slice_fusion.6
  64.0 1.0 convolution_convert_fusion.1
  65.0 1.6 copy-done.2
  66.8 1.9 collective-permute-start.3
  68.8 1.3 collective-permute-start.4
  70.1 1.1 constant_dynamic-update-slice_fusion.3
  71.2 2.5 collective-permute-done.4
  73.8 1.0 pad_maximum_fusion.4
  74.8 4.2 %collective-permute-start.5 = (bf16[14,3,2176]{2,1,0:T(4,128)(2,1)}, bf16[14,3,2176]{2,1,0:T(4,128)(2,1)}, u32[]{:S(2)}, u32[]{:S(2)}) collective-permute-start(bf16[14,3,2176]{2,1,0:T(4,128)(2,1)} %get-tuple-element.62), channel_id=1, source_target_pairs={{0,1},{1,2},{2,3},{4,5},{5,6},{6,7},{8,9},{9,10},{10,11},{12,13},{... | collective-permute-start | bytes 548360 | tf_op jit(solution)/shard_map/ppermute | solution.py:18
  78.9 1.5 collective-permute-start.6
  80.4 1.4 convolution_convert_fusion.4
  82.7 4.6 %collective-permute-done.6 = bf16[14,3,2176]{2,1,0:T(4,128)(2,1)} collective-permute-done((bf16[14,3,2176]{2,1,0:T(4,128)(2,1)}, bf16[14,3,2176]{2,1,0:T(4,128)(2,1)}, u32[]{:S(2)}, u32[]{:S(2)}) %collective-permute-start.6) | collective-permute-done | bytes 182816 | tf_op jit(solution)/shard_map/ppermute | solution.py:19
  87.3 3.0 pad_maximum_fusion
  90.3 2.5 reshape.396
  92.7 2.4 fusion.60
  95.2 1.0 compare_reduce_fusion
  96.2 1.4 copy.29
  97.6 2.2 copy.32
  100.1 1.8 fusion.62
  103.1 1.8 multiply_reduce_fusion
  104.9 2.4 convolution_bitcast_fusion.1
  107.3 0.9 subtract_multiply_fusion
  108.2 3.2 copy.35
  111.4 3.0 reshape.404
  114.4 3.1 multiply_bitcast_fusion
  117.5 3.2 copy.34
  120.6 3.0 reshape.403
  123.6 1.5 constant_dynamic-update-slice_fusion.1
  125.5 1.6 copy-done.5
  127.1 1.1 fusion.59
  128.2 5.6 %collective-permute-start.10 = (f32[3,22,2048]{2,1,0:T(8,128)}, f32[3,22,2048]{2,1,0:T(8,128)}, u32[]{:S(2)}, u32[]{:S(2)}) collective-permute-start(f32[3,22,2048]{2,1,0:T(8,128)} %get-tuple-element.59), channel_id=1, source_target_pairs={{0,4},{4,8},{8,12},{1,5},{5,9},{9,13},{2,6},{6,10},{10,14},{3,7},{... | collective-permute-start | bytes 1622024 | tf_op jit(solution)/shard_map/ppermute | solution.py:27
  133.8 2.1 convolution_convert_fusion.2
  136.5 1.6 collective-permute-start.11
  138.2 1.5 fusion.11
  139.6 1.2 slice.181
  140.9 2.3 copy.37
  143.2 5.5 %dot_general.55 = f32[4,4,39424]{2,1,0:T(4,128)} reshape(f32[16,128,308]{2,1,0:T(8,128)} %copy.37) | data formatting | bytes 5046272 | tf_op jit(solution)/shard_map/dot_general | solution.py:134
  148.7 1.3 fusion.38
  150.1 1.4 fusion.37
  152.3 3.5 %collective-permute-start.12 = (bf16[8,3,2048]{2,1,0:T(4,128)(2,1)S(1)}, bf16[8,3,2048]{2,1,0:T(4,128)(2,1)}, u32[]{:S(2)}, u32[]{:S(2)}) collective-permute-start(bf16[8,3,2048]{2,1,0:T(4,128)(2,1)S(1)} %get-tuple-element.65), channel_id=1, source_target_pairs={{0,1},{1,2},{2,3},{4,5},{5,6},{6,7},{8,9},{9,10},{10,11},{12,13},{... | collective-permute-start | bytes 294920 | tf_op jit(solution)/shard_map/ppermute | solution.py:27
  155.8 3.4 fusion.12
  159.9 1.1 concatenate.42
  161.8 1.3 collective-permute-start.13
  163.1 1.0 slice_add_fusion.3
  164.9 5.2 %collective-permute-done.13 = bf16[8,3,2048]{2,1,0:T(4,128)(2,1)S(1)} collective-permute-done((bf16[8,3,2048]{2,1,0:T(4,128)(2,1)}, bf16[8,3,2048]{2,1,0:T(4,128)(2,1)S(1)}, u32[]{:S(2)}, u32[]{:S(2)}) %collective-permute-start.13) | collective-permute-done | bytes 98336 | tf_op jit(solution)/shard_map/ppermute | solution.py:27
  171.0 5.3 %fusion.44 = (bf16[1024]{0:T(1024)(128)(2,1)S(1)}, f32[8,16]{1,0:T(8,128)S(1)}, f32[8,16]{1,0:T(8,128)S(1)}, f32[8,16,1024]{2,1,0:T(8,128)S(1)}) fusion(bf16[8,16,1024]{2,1,0:T(8,128)(2,1)S(1)} %copy-done.11, f32[8,16]{1,0:T(8,128)S(1)} %add_rsqrt_fusion, f32[8,16]{1,0:T(8,128)S(1)} %broadcast_multiply_fusion.2, f32[1024]{0:T(1024)S(1)} %copy-done.27, ...), kind=kOutput, calls=%fused_computation.61 | convolution fusion | flops 808057600 | bytes 7872512 | tf_op jit(solution)/shard_map/dot_general | solution.py:170
  176.5 4.7 %convolution_convert_fusion = bf16[1024,3200]{1,0:T(8,128)(2,1)} fusion(bf16[128,1024]{1,0:T(8,128)(2,1)S(1)} %bitcast.61, bf16[128,2048]{1,0:T(8,128)(2,1)S(1)} %bitcast.68, bf16[128,1024]{1,0:T(8,128)(2,1)S(1)} %copy.36), kind=kOutput, calls=%fused_computation.4 | convolution fusion | flops 845004800 | bytes 7602176 | tf_op jit(solution)/shard_map/dot_general | solution.py:189
  181.2 0.9 maximum_dynamic-update-slice_fusion
  182.2 58.7 %reduce-scatter.3.cloned.1.call-done = bf16[256,3200]{1,0:T(8,128)(2,1)} async-done(((bf16[1024,3200]{1,0:T(8,128)(2,1)}), bf16[256,3200]{1,0:T(8,128)(2,1)}) %reduce-scatter.3.cloned.1.call-update) | async-done | bytes 1638416 | tf_op jit(solution)/shard_map/reduce_scatter | solution.py:194
  241.0 1.1 fusion.43
  242.0 90.9 %all-reduce.5.cloned.1.call-done = (bf16[256,3200]{1,0:T(8,128)(2,1)}, bf16[256,1024]{1,0:T(8,128)(2,1)}) async-done(((bf16[256,3200]{1,0:T(8,128)(2,1)}, bf16[256,1024]{1,0:T(8,128)(2,1)}), (bf16[256,3200]{1,0:T(8,128)(2,1)}, bf16[256,1024]{1,0:T(8,128)(2,1)})) %all-reduce.5.cloned.1.call-update) | async-done | bytes 2162704 | tf_op jit(solution)/shard_map/psum | solution.py:194
  333.0 1.8 convert_element_type.80
  334.9 2.0 slice.191
  338.2 1.1 convert_element_type.82
  (131 shorter events, 15.7 us)
Async XLA Ops:
  7.2 6.5 %copy-start = (f32[16,49]{1,0:T(8,128)S(1)}, f32[16,49]{1,0:T(8,128)}, u32[]{:S(2)}) copy-start(f32[16,49]{1,0:T(8,128)} %param.20) | copy-start | bytes 9412
  7.2 175.0 %reduce-scatter.5.cloned.1.call-start = ((), (), s32[]{:S(2)}) async-start(), calls=%async_computation.3 | async-start | bytes 2621440 | tf_op jit(solution)/shard_map/reduce_scatter | solution.py:123
  7.2 38.6 %collective-permute-start = (bf16[256,3072]{1,0:T(8,128)(2,1)}, bf16[256,3072]{1,0:T(8,128)(2,1)}, u32[]{:S(2)}, u32[]{:S(2)}) collective-permute-start(bf16[256,3072]{1,0:T(8,128)(2,1)} %param.17), channel_id=1, source_target_pairs={{0,8},{4,12},{8,0},{12,4},{1,9},{5,13},{9,1},{13,5},{2,10},{6,14},... | collective-permute-start | bytes 4718600 | tf_op jit(solution)/shard_map/ppermute | solution.py:36
  10.3 50.5 %collective-permute-start.1 = (bf16[256,3072]{1,0:T(8,128)(2,1)}, bf16[256,3072]{1,0:T(8,128)(2,1)}, u32[]{:S(2)}, u32[]{:S(2)}) collective-permute-start(bf16[256,3072]{1,0:T(8,128)(2,1)} %param.17), channel_id=1, source_target_pairs={{0,4},{4,0},{8,12},{12,8},{1,5},{5,1},{9,13},{13,9},{2,6},{6,2},{1... | collective-permute-start | bytes 4718600 | tf_op jit(solution)/shard_map/ppermute | solution.py:39
  10.3 47.3 %collective-permute-start.7 = (bf16[256,1024]{1,0:T(8,128)(2,1)}, bf16[256,1024]{1,0:T(8,128)(2,1)}, u32[]{:S(2)}, u32[]{:S(2)}) collective-permute-start(bf16[256,1024]{1,0:T(8,128)(2,1)} %param.18), channel_id=1, source_target_pairs={{0,8},{4,12},{8,0},{12,4},{1,9},{5,13},{9,1},{13,5},{2,10},{6,14},... | collective-permute-start | bytes 1572872 | tf_op jit(solution)/shard_map/ppermute | solution.py:36
  10.4 59.6 %collective-permute-start.8 = (bf16[256,1024]{1,0:T(8,128)(2,1)}, bf16[256,1024]{1,0:T(8,128)(2,1)}, u32[]{:S(2)}, u32[]{:S(2)}) collective-permute-start(bf16[256,1024]{1,0:T(8,128)(2,1)} %param.18), channel_id=1, source_target_pairs={{0,4},{4,0},{8,12},{12,8},{1,5},{5,1},{9,13},{13,9},{2,6},{6,2},{1... | collective-permute-start | bytes 1572872 | tf_op jit(solution)/shard_map/ppermute | solution.py:39
  13.2 32.6 %copy-start.10 = (bf16[8,16,1024]{2,1,0:T(8,128)(2,1)S(1)}, bf16[8,16,1024]{2,1,0:T(8,128)(2,1)}, u32[]{:S(2)}) copy-start(bf16[8,16,1024]{2,1,0:T(8,128)(2,1)} %param.15) | copy-start | bytes 786436
  13.2 32.6 %copy-start.26 = (f32[1024]{0:T(1024)S(1)}, f32[1024]{0:T(1024)}, u32[]{:S(2)}) copy-start(f32[1024]{0:T(1024)} %param.19) | copy-start | bytes 12292
  13.6 32.4 %copy-start.30 = (s32[8,16]{1,0:T(8,128)S(1)}, s32[8,16]{1,0:T(8,128)}, u32[]{:S(2)}) copy-start(s32[8,16]{1,0:T(8,128)} %param.21) | copy-start | bytes 1540
  45.8 16.6 %collective-permute-start.2 = (bf16[256,3072]{1,0:T(8,128)(2,1)}, bf16[256,3072]{1,0:T(8,128)(2,1)}, u32[]{:S(2)}, u32[]{:S(2)}) collective-permute-start(bf16[256,3072]{1,0:T(8,128)(2,1)} %collective-permute-done), channel_id=1, source_target_pairs={{0,4},{4,0},{8,12},{12,8},{1,5},{5,1},{9,13},{13,9},{2,6},{6,2},{1... | collective-permute-start | bytes 4718600 | tf_op jit(solution)/shard_map/ppermute | solution.py:39
  46.0 18.0 %copy-start.8 = (bf16[8,16,1024]{2,1,0:T(8,128)(2,1)}, bf16[8,16,1024]{2,1,0:T(8,128)(2,1)S(1)}, u32[]{:S(2)}) copy-start(bf16[8,16,1024]{2,1,0:T(8,128)(2,1)S(1)} %fusion.39) | copy-start | bytes 786436
  53.2 2.7 copy-start.23
  55.9 1.4 copy-start.17
  57.5 13.6 %collective-permute-start.9 = (bf16[256,1024]{1,0:T(8,128)(2,1)}, bf16[256,1024]{1,0:T(8,128)(2,1)S(1)}, u32[]{:S(2)}, u32[]{:S(2)}) collective-permute-start(bf16[256,1024]{1,0:T(8,128)(2,1)} %collective-permute-done.7), channel_id=1, source_target_pairs={{0,4},{4,0},{8,12},{12,8},{1,5},{5,1},{9,13},{13,9},{2,6},{6,2},{1... | collective-permute-start | bytes 1572872 | tf_op jit(solution)/shard_map/ppermute | solution.py:39
  64.0 2.6 copy-start.2
  64.0 2.7 copy-start.29
  66.6 13.8 %copy-start.13 = (bf16[8,16,1024]{2,1,0:T(8,128)(2,1)S(1)}, bf16[8,16,1024]{2,1,0:T(8,128)(2,1)}, u32[]{:S(2)}) copy-start(bf16[8,16,1024]{2,1,0:T(8,128)(2,1)} %param.16) | copy-start | bytes 786436
  66.8 4.4 %collective-permute-start.3 = (bf16[3,16,2176]{2,1,0:T(8,128)(2,1)S(1)}, bf16[3,16,2176]{2,1,0:T(8,128)(2,1)S(1)}, u32[]{:S(2)}, u32[]{:S(2)}) collective-permute-start(bf16[3,16,2176]{2,1,0:T(8,128)(2,1)S(1)} %get-tuple-element.66), channel_id=1, source_target_pairs={{0,4},{4,8},{8,12},{1,5},{5,9},{9,13},{2,6},{6,10},{10,14},{3,7},{... | collective-permute-start | bytes 626696 | tf_op jit(solution)/shard_map/ppermute | solution.py:18
  68.8 5.0 %collective-permute-start.4 = (bf16[3,16,2176]{2,1,0:T(8,128)(2,1)S(1)}, bf16[3,16,2176]{2,1,0:T(8,128)(2,1)S(1)}, u32[]{:S(2)}, u32[]{:S(2)}) collective-permute-start(bf16[3,16,2176]{2,1,0:T(8,128)(2,1)S(1)} %get-tuple-element.67), channel_id=1, source_target_pairs={{4,0},{8,4},{12,8},{5,1},{9,5},{13,9},{6,2},{10,6},{14,10},{7,3},{... | collective-permute-start | bytes 626696 | tf_op jit(solution)/shard_map/ppermute | solution.py:19
  71.2 9.2 %copy-start.19 = (bf16[3,16,2176]{2,1,0:T(8,128)(2,1)}, bf16[3,16,2176]{2,1,0:T(8,128)(2,1)S(1)}, u32[]{:S(2)}) copy-start(bf16[3,16,2176]{2,1,0:T(8,128)(2,1)S(1)} %collective-permute-done.3) | copy-start | bytes 626692
  73.8 8.1 %copy-start.20 = (bf16[3,16,2176]{2,1,0:T(8,128)(2,1)}, bf16[3,16,2176]{2,1,0:T(8,128)(2,1)S(1)}, u32[]{:S(2)}) copy-start(bf16[3,16,2176]{2,1,0:T(8,128)(2,1)S(1)} %collective-permute-done.4) | copy-start | bytes 626692
  74.8 8.0 %collective-permute-start.5 = (bf16[14,3,2176]{2,1,0:T(4,128)(2,1)}, bf16[14,3,2176]{2,1,0:T(4,128)(2,1)}, u32[]{:S(2)}, u32[]{:S(2)}) collective-permute-start(bf16[14,3,2176]{2,1,0:T(4,128)(2,1)} %get-tuple-element.62), channel_id=1, source_target_pairs={{0,1},{1,2},{2,3},{4,5},{5,6},{6,7},{8,9},{9,10},{10,11},{12,13},{... | collective-permute-start | bytes 548360 | tf_op jit(solution)/shard_map/ppermute | solution.py:18
  78.9 8.4 %collective-permute-start.6 = (bf16[14,3,2176]{2,1,0:T(4,128)(2,1)}, bf16[14,3,2176]{2,1,0:T(4,128)(2,1)}, u32[]{:S(2)}, u32[]{:S(2)}) collective-permute-start(bf16[14,3,2176]{2,1,0:T(4,128)(2,1)} %get-tuple-element.63), channel_id=1, source_target_pairs={{1,0},{2,1},{3,2},{5,4},{6,5},{7,6},{9,8},{10,9},{11,10},{13,12},{... | collective-permute-start | bytes 548360 | tf_op jit(solution)/shard_map/ppermute | solution.py:19
  92.7 7.1 %copy-start.28 = (s32[308]{0:T(512)S(1)}, s32[308]{0:T(512)}, u32[]{:S(2)}) copy-start(s32[308]{0:T(512)} %iota.114) | copy-start | bytes 3700
  92.7 7.1 %copy-start.31 = (s32[128]{0:T(128)S(1)}, s32[128]{0:T(128)}, u32[]{:S(2)}) copy-start(s32[128]{0:T(128)} %iota.111) | copy-start | bytes 1540
  92.7 7.1 %copy-start.32 = (s32[128]{0:T(128)S(1)}, s32[128]{0:T(128)}, u32[]{:S(2)}) copy-start(s32[128]{0:T(128)} %iota.117) | copy-start | bytes 1540
  102.0 1.1 copy-start.21
  102.0 1.2 copy-start.24
  123.6 1.8 copy-start.7
  125.4 8.4 %copy-start.14 = (bf16[8,16,1024]{2,1,0:T(8,128)(2,1)S(1)}, bf16[8,16,1024]{2,1,0:T(8,128)(2,1)}, u32[]{:S(2)}) copy-start(bf16[8,16,1024]{2,1,0:T(8,128)(2,1)} %param.16) | copy-start | bytes 786436
  125.4 8.4 %copy-start.25 = (bf16[16,64,128]{2,1,0:T(8,128)(2,1)S(1)}, bf16[16,64,128]{2,1,0:T(8,128)(2,1)}, u32[]{:S(2)}) copy-start(bf16[16,64,128]{2,1,0:T(8,128)(2,1)} %get-tuple-element.71) | copy-start | bytes 786436
  125.5 1.6 copy-start.5
  128.2 20.5 %collective-permute-start.10 = (f32[3,22,2048]{2,1,0:T(8,128)}, f32[3,22,2048]{2,1,0:T(8,128)}, u32[]{:S(2)}, u32[]{:S(2)}) collective-permute-start(f32[3,22,2048]{2,1,0:T(8,128)} %get-tuple-element.59), channel_id=1, source_target_pairs={{0,4},{4,8},{8,12},{1,5},{5,9},{9,13},{2,6},{6,10},{10,14},{3,7},{... | collective-permute-start | bytes 1622024 | tf_op jit(solution)/shard_map/ppermute | solution.py:27
  135.9 105.1 %reduce-scatter.3.cloned.1.call-start = ((), (), s32[]{:S(2)}) async-start(), calls=%async_computation.2 | async-start | bytes 8192000 | tf_op jit(solution)/shard_map/reduce_scatter | solution.py:194
  135.9 3.7 %copy-start.6 = (f32[14,22,2048]{2,1,0:T(8,128)S(1)}, f32[14,22,2048]{2,1,0:T(8,128)}, u32[]{:S(2)}) copy-start(f32[14,22,2048]{2,1,0:T(8,128)} %copy-done.5) | copy-start | bytes 7569412
  136.5 13.5 %collective-permute-start.11 = (f32[3,22,2048]{2,1,0:T(8,128)}, f32[3,22,2048]{2,1,0:T(8,128)}, u32[]{:S(2)}, u32[]{:S(2)}) collective-permute-start(f32[3,22,2048]{2,1,0:T(8,128)} %get-tuple-element.58), channel_id=1, source_target_pairs={{4,0},{8,4},{12,8},{5,1},{9,5},{13,9},{6,2},{10,6},{14,10},{7,3},{... | collective-permute-start | bytes 1622024 | tf_op jit(solution)/shard_map/ppermute | solution.py:27
  143.2 5.5 %copy-start.3 = (f32[8,22,2048]{2,1,0:T(8,128)S(1)}, f32[8,22,2048]{2,1,0:T(8,128)}, u32[]{:S(2)}) copy-start(f32[8,22,2048]{2,1,0:T(8,128)} %slice.181) | copy-start | bytes 4325380
  150.0 5.8 %copy-start.12 = (f32[4,4,39424]{2,1,0:T(4,128)S(1)}, f32[4,4,39424]{2,1,0:T(4,128)}, u32[]{:S(2)}) copy-start(f32[4,4,39424]{2,1,0:T(4,128)} %dot_general.55) | copy-start | bytes 7569412
  151.4 7.9 %copy-start.16 = (bf16[16,64,128]{2,1,0:T(8,128)(2,1)S(1)}, bf16[16,64,128]{2,1,0:T(8,128)(2,1)}, u32[]{:S(2)}) copy-start(bf16[16,64,128]{2,1,0:T(8,128)(2,1)} %fusion.11) | copy-start | bytes 786436
  152.3 10.8 %collective-permute-start.12 = (bf16[8,3,2048]{2,1,0:T(4,128)(2,1)S(1)}, bf16[8,3,2048]{2,1,0:T(4,128)(2,1)}, u32[]{:S(2)}, u32[]{:S(2)}) collective-permute-start(bf16[8,3,2048]{2,1,0:T(4,128)(2,1)S(1)} %get-tuple-element.65), channel_id=1, source_target_pairs={{0,1},{1,2},{2,3},{4,5},{5,6},{6,7},{8,9},{9,10},{10,11},{12,13},{... | collective-permute-start | bytes 294920 | tf_op jit(solution)/shard_map/ppermute | solution.py:27
  161.7 9.3 %copy-start.11 = (bf16[8,16,1024]{2,1,0:T(8,128)(2,1)S(1)}, bf16[8,16,1024]{2,1,0:T(8,128)(2,1)}, u32[]{:S(2)}) copy-start(bf16[8,16,1024]{2,1,0:T(8,128)(2,1)} %param.15) | copy-start | bytes 786436
  161.7 9.3 %copy-start.27 = (f32[1024]{0:T(1024)S(1)}, f32[1024]{0:T(1024)}, u32[]{:S(2)}) copy-start(f32[1024]{0:T(1024)} %param.19) | copy-start | bytes 12292
  161.8 8.3 %collective-permute-start.13 = (bf16[8,3,2048]{2,1,0:T(4,128)(2,1)}, bf16[8,3,2048]{2,1,0:T(4,128)(2,1)S(1)}, u32[]{:S(2)}, u32[]{:S(2)}) collective-permute-start(bf16[8,3,2048]{2,1,0:T(4,128)(2,1)} %get-tuple-element.64), channel_id=1, source_target_pairs={{1,0},{2,1},{3,2},{5,4},{6,5},{7,6},{9,8},{10,9},{11,10},{13,12},{... | collective-permute-start | bytes 294920 | tf_op jit(solution)/shard_map/ppermute | solution.py:27
  171.0 5.5 %copy-start.9 = (bf16[8,16,1024]{2,1,0:T(8,128)(2,1)S(1)}, bf16[8,16,1024]{2,1,0:T(8,128)(2,1)}, u32[]{:S(2)}) copy-start(bf16[8,16,1024]{2,1,0:T(8,128)(2,1)} %copy-done.8) | copy-start | bytes 786436
  176.5 4.7 %copy-start.18 = (bf16[4,256,49]{2,1,0:T(8,128)(2,1)S(1)}, bf16[4,256,49]{2,1,0:T(8,128)(2,1)}, u32[]{:S(2)}) copy-start(bf16[4,256,49]{2,1,0:T(8,128)(2,1)} %pad.18) | copy-start | bytes 301060
  176.5 4.7 %copy-start.33 = (bf16[128]{0:T(256)(128)(2,1)S(1)}, bf16[128]{0:T(256)(128)(2,1)}, u32[]{:S(2)}) copy-start(bf16[128]{0:T(256)(128)(2,1)} %pad.21.clone) | copy-start | bytes 772
  182.1 58.9 %copy-start.15 = (bf16[8,16,1024]{2,1,0:T(8,128)(2,1)S(1)}, bf16[8,16,1024]{2,1,0:T(8,128)(2,1)}, u32[]{:S(2)}) copy-start(bf16[8,16,1024]{2,1,0:T(8,128)(2,1)} %param.16) | copy-start | bytes 786436
  182.1 150.8 %all-reduce.5.cloned.1.call-start = ((), (), s32[]{:S(2)}) async-start(), calls=%async_computation.4 | async-start | bytes 4325376 | tf_op jit(solution)/shard_map/psum | solution.py:194
  333.0 1.9 copy-start.4
  333.0 6.4 %copy-start.1 = (f32[16,49]{1,0:T(8,128)S(1)}, f32[16,49]{1,0:T(8,128)}, u32[]{:S(2)}) copy-start(f32[16,49]{1,0:T(8,128)} %param.20) | copy-start | bytes 9412
  334.9 3.4 copy-start.22
Sparse Core Ops, SparseCore 0:
  136.0 30.1 reduce-scatter.4
  182.2 58.6 reduce-scatter.2
  243.4 89.5 all-reduce.4

commit v5 on v4

--- a/solution.py
+++ b/solution.py
@@ -62,16 +62,16 @@
     )
 
 
-def window_tables(rows, cols, reach):
+def window_tables(rows, cols, reach, key_cols):
     side = 2 * reach + 1
-    shape = (rows, cols, rows + 2 * reach, cols + 2 * reach)
+    shape = (rows, cols, rows + 2 * reach, key_cols)
     row_gap = lax.broadcasted_iota(jnp.int32, shape, 2) - lax.broadcasted_iota(jnp.int32, shape, 0)
     col_gap = lax.broadcasted_iota(jnp.int32, shape, 3) - lax.broadcasted_iota(jnp.int32, shape, 1)
     inside = (row_gap >= 0) & (row_gap < side) & (col_gap >= 0) & (col_gap < side)
     offset_id = jnp.where(inside, row_gap * side + col_gap, -1)
     centre = (row_gap == reach) & (col_gap == reach)
     nq = rows * cols
-    nk = (rows + 2 * reach) * (cols + 2 * reach)
+    nk = (rows + 2 * reach) * key_cols
     offset_id = offset_id.reshape(nq * nk)
     one_hot = (
         offset_id[None, :] == lax.broadcasted_iota(jnp.int32, (side * side, nq * nk), 0)
@@ -85,7 +85,8 @@
     hdim = width // heads
     reach = RAD
     ext_rows, ext_cols = rows + 2 * reach, cols + 2 * reach
-    nq, nk = rows * cols, ext_rows * ext_cols
+    key_cols = ext_cols + (-ext_cols) % 8
+    nq, nk = rows * cols, ext_rows * key_cols
     scale = float(hdim) ** (-0.5)
     full_qkv, full_out = gathered_rows((qkv_weight, out_weight))
     normed_features, standardized_input, inverse_deviation = apply_layer_norm(
@@ -96,13 +97,14 @@
     query = joined[:, :width]
     flags = jnp.broadcast_to(valid_mask.astype(jnp.bfloat16)[:, :, None], (rows, cols, 128))
     kv = jnp.concatenate([joined[:, width:].reshape(rows, cols, 2 * width), flags], axis=-1)
-    kv_ext = extended_2(kv, (("row", 0), ("col", 1)), reach).reshape(nk, 2 * width + 128)
+    kv_ext = extended_2(kv, (("row", 0), ("col", 1)), reach)
+    kv_ext = jnp.pad(kv_ext, ((0, 0), (0, key_cols - ext_cols), (0, 0))).reshape(nk, 2 * width + 128)
     mask_ext = kv_ext[:, 2 * width]
     q3 = query.reshape(nq, heads, hdim)
     k3 = kv_ext[:, :width].reshape(nk, heads, hdim)
     v3 = kv_ext[:, width : 2 * width].reshape(nk, heads, hdim)
 
-    inside, centre, one_hot = window_tables(rows, cols, reach)
+    inside, centre, one_hot = window_tables(rows, cols, reach, key_cols)
     allowed = inside & ((mask_ext[None, :] == 1.0) | centre)
     bias_full = jnp.dot(pos_bias, one_hot, precision=HIGHEST).reshape(heads, nq, nk)
     raw = jnp.einsum("phd,khd->hpk", q3, k3, preferred_element_type=jnp.float32)
@@ -148,9 +150,9 @@
         preferred_element_type=jnp.float32,
     )
     buffer = jnp.concatenate(
-        [key_ext_grad.reshape(ext_rows, ext_cols, width), value_ext_grad.reshape(ext_rows, ext_cols, width)],
+        [key_ext_grad.reshape(ext_rows, key_cols, width), value_ext_grad.reshape(ext_rows, key_cols, width)],
         axis=-1,
-    )
+    )[:, :ext_cols]
     from_below = passed_along(buffer[:reach], "row", -1)
     from_above = passed_along(buffer[reach + rows :], "row", 1)
     middle = buffer[reach : reach + rows]

time: 347 us -> 345 us (level)
    reshape x3 -> x2, local copies, waits for them, and re-layouts: 8.43 us -> 6.07 us  [the longest x1 3.05 us: body(): value_ext_grad.reshape(ext_rows, key_cols, width)]
where the time goes in v5:
time: 345 us; the launch traced here: 344 us
  waiting for transfers between devices  192 us (56%)
  local copies, waits for them, and re-layouts  61.9 us (18%)
  matrix products  33 us (10%)
  starting transfers between devices  24.4 us (7%)
  other arithmetic  18 us (5%)
  between operations  14.5 us (4%)
    psum x1, waiting for transfers between devices, body(): lax.psum(lax.psum_scatter(big, 'row', scatter_dimension=0, tiled=True), '...  90.9 us
    reduce_scatter x1, waiting for transfers between devices, body(): lax.psum_scatter(big, 'row', scatter_dimension=0, tiled=True)  59.4 us
    ppermute x2, waiting for transfers between devices, gathered_rows(): held.append((lax.ppermute(shards, 'row', pairs), (index - step) % count))  28.6 us
    ppermute x4, starting transfers between devices, passed_along(): lax.ppermute(value, axis, [(source, source + steps) for source in range(f...  11.3 us
    dynamic_update_slice x8, local copies, waits for them, and re-layouts, gathered_rows(): lax.dynamic_update_slice_in_dim(full, piece[leaf], block * size, axis=0)  7.2 us
    ppermute x2, waiting for transfers between devices, extended_2(): after = lax.ppermute(first, axis, down)  7.1 us
  transfers between devices with their start and end apart: 17, of which 6 were waited for; matrix products, arithmetic and copies ran while one was open for 19% of the time, Pallas kernels for 0%

profile of v5, /device:TPU:0, one launch (start us, length us, event | category | flops | bytes accessed | tf_op | source)
XLA Modules:
  0.0 344.2 jit_solution(5494801014798501262)
XLA Ops:
  7.2 3.0 collective-permute-start
  10.8 1.1 convert_reduce_fusion
  11.8 1.1 fusion.56
  13.8 3.4 convolution_bitcast_fusion
  17.2 28.6 %collective-permute-done = bf16[256,3072]{1,0:T(8,128)(2,1)} collective-permute-done((bf16[256,3072]{1,0:T(8,128)(2,1)}, bf16[256,3072]{1,0:T(8,128)(2,1)}, u32[]{:S(2)}, u32[]{:S(2)}) %collective-permute-start) | collective-permute-done | bytes 1572896 | tf_op jit(solution)/shard_map/ppermute | solution.py:36
  49.3 3.8 %reshape.399 = f32[16,128,336]{2,1,0:T(8,128)} reshape(f32[16,43008]{1,0:T(8,128)S(1)} %convolution_bitcast_fusion) | data formatting | bytes 5505024 | tf_op jit(solution)/shard_map/reshape | solution.py:109
  53.1 2.4 copy.31
  58.0 1.1 constant_dynamic-update-slice_fusion.4
  59.1 1.6 constant_dynamic-update-slice_fusion.8
  60.7 1.6 constant_dynamic-update-slice_fusion.7
  62.3 1.6 constant_dynamic-update-slice_fusion.6
  64.0 1.0 convolution_convert_fusion.1
  65.0 1.6 copy-done.2
  66.8 1.9 collective-permute-start.3
  68.7 1.3 collective-permute-start.4
  70.0 1.1 constant_dynamic-update-slice_fusion.3
  71.2 2.5 collective-permute-done.4
  73.7 1.0 pad_maximum_fusion.3
  74.7 4.2 %collective-permute-start.5 = (bf16[14,3,2176]{2,1,0:T(4,128)(2,1)}, bf16[14,3,2176]{2,1,0:T(4,128)(2,1)}, u32[]{:S(2)}, u32[]{:S(2)}) collective-permute-start(bf16[14,3,2176]{2,1,0:T(4,128)(2,1)} %get-tuple-element.62), channel_id=1, source_target_pairs={{0,1},{1,2},{2,3},{4,5},{5,6},{6,7},{8,9},{9,10},{10,11},{12,13},{... | collective-permute-start | bytes 548360 | tf_op jit(solution)/shard_map/ppermute | solution.py:18
  78.9 1.5 collective-permute-start.6
  80.4 1.4 convolution_convert_fusion.4
  81.8 0.8 copy.30
  82.7 4.6 %collective-permute-done.6 = bf16[14,3,2176]{2,1,0:T(4,128)(2,1)} collective-permute-done((bf16[14,3,2176]{2,1,0:T(4,128)(2,1)}, bf16[14,3,2176]{2,1,0:T(4,128)(2,1)}, u32[]{:S(2)}, u32[]{:S(2)}) %collective-permute-start.6) | collective-permute-done | bytes 182816 | tf_op jit(solution)/shard_map/ppermute | solution.py:19
  87.3 3.1 fusion.18
  90.3 1.3 fusion.71
  92.3 1.4 copy.29
  93.7 2.3 copy.32
  96.0 0.9 fusion.61
  96.9 1.8 fusion.73
  99.9 1.8 multiply_reduce_fusion
  101.7 2.4 convolution_bitcast_fusion.1
  104.1 0.8 subtract_multiply_fusion
  104.9 3.1 copy.35
  108.1 3.0 reshape.404
  111.1 3.1 multiply_bitcast_fusion
  114.2 3.1 copy.34
  117.4 3.0 reshape.403
  120.4 1.5 constant_dynamic-update-slice_fusion.1
  122.3 1.6 copy-done.5
  123.9 1.1 fusion.70
  125.0 5.6 %collective-permute-start.10 = (f32[3,22,2048]{2,1,0:T(8,128)}, f32[3,22,2048]{2,1,0:T(8,128)}, u32[]{:S(2)}, u32[]{:S(2)}) collective-permute-start(f32[3,22,2048]{2,1,0:T(8,128)} %get-tuple-element.59), channel_id=1, source_target_pairs={{0,4},{4,8},{8,12},{1,5},{5,9},{9,13},{2,6},{6,10},{10,14},{3,7},{... | collective-permute-start | bytes 1622024 | tf_op jit(solution)/shard_map/ppermute | solution.py:27
  130.6 2.1 convolution_convert_fusion.2
  133.3 1.6 collective-permute-start.11
  135.0 1.5 fusion.22
  136.4 1.3 slice.185
  137.7 2.3 copy.37
  140.0 5.7 %dot_general.55 = f32[4,4,43008]{2,1,0:T(4,128)} reshape(f32[16,128,336]{2,1,0:T(8,128)} %copy.37) | data formatting | bytes 5505024 | tf_op jit(solution)/shard_map/dot_general | solution.py:136
  145.8 1.3 fusion.49
  147.1 1.4 fusion.48
  149.4 2.8 collective-permute-start.12
  152.2 3.7 %fusion.23 = bf16[4,4,49]{2,1,0:T(4,128)(2,1)S(1)} fusion(f32[4,4,43008]{2,1,0:T(4,128)S(1)} %copy-done.12, s32[43008]{0:T(1024)S(1)} %copy-done.19), kind=kOutput, calls=%fused_computation.37 | convolution fusion | flops 204417808 | bytes 2926112 | tf_op jit(solution)/shard_map/dot_general | solution.py:136
  156.6 1.1 concatenate.42
  158.5 1.3 collective-permute-start.13
  160.6 6.2 %collective-permute-done.13 = bf16[8,3,2048]{2,1,0:T(4,128)(2,1)} collective-permute-done((bf16[8,3,2048]{2,1,0:T(4,128)(2,1)}, bf16[8,3,2048]{2,1,0:T(4,128)(2,1)}, u32[]{:S(2)}, u32[]{:S(2)}) %collective-permute-start.13) | collective-permute-done | bytes 98336 | tf_op jit(solution)/shard_map/ppermute | solution.py:27
  166.9 1.0 slice_add_fusion.2
  168.7 5.2 %fusion.55 = (bf16[1024]{0:T(1024)(128)(2,1)S(1)}, f32[8,16]{1,0:T(8,128)S(1)}, f32[8,16]{1,0:T(8,128)S(1)}, f32[8,16,1024]{2,1,0:T(8,128)S(1)}) fusion(bf16[8,16,1024]{2,1,0:T(8,128)(2,1)S(1)} %copy-done.11, f32[8,16]{1,0:T(8,128)S(1)} %add_rsqrt_fusion, f32[8,16]{1,0:T(8,128)S(1)} %broadcast_multiply_fusion.2, f32[1024]{0:T(1024)S(1)} %copy-done.30, ...), kind=kOutput, calls=%fused_computation.72 | convolution fusion | flops 808057600 | bytes 7872512 | tf_op jit(solution)/shard_map/dot_general | solution.py:172
  174.2 4.7 %convolution_convert_fusion = bf16[1024,3200]{1,0:T(8,128)(2,1)} fusion(bf16[128,1024]{1,0:T(8,128)(2,1)S(1)} %bitcast.64, bf16[128,2048]{1,0:T(8,128)(2,1)S(1)} %bitcast.71, bf16[128,1024]{1,0:T(8,128)(2,1)S(1)} %copy.36), kind=kOutput, calls=%fused_computation.4 | convolution fusion | flops 845004800 | bytes 7602176 | tf_op jit(solution)/shard_map/dot_general | solution.py:191
  178.9 0.9 maximum_dynamic-update-slice_fusion
  179.9 59.4 %reduce-scatter.3.cloned.1.call-done = bf16[256,3200]{1,0:T(8,128)(2,1)} async-done(((bf16[1024,3200]{1,0:T(8,128)(2,1)}), bf16[256,3200]{1,0:T(8,128)(2,1)}) %reduce-scatter.3.cloned.1.call-update) | async-done | bytes 1638416 | tf_op jit(solution)/shard_map/reduce_scatter | solution.py:196
  239.3 1.1 fusion.54
  240.4 90.9 %all-reduce.6.cloned.1.call-done = (bf16[256,3200]{1,0:T(8,128)(2,1)}, bf16[256,1024]{1,0:T(8,128)(2,1)}) async-done(((bf16[256,3200]{1,0:T(8,128)(2,1)}, bf16[256,1024]{1,0:T(8,128)(2,1)}), (bf16[256,3200]{1,0:T(8,128)(2,1)}, bf16[256,1024]{1,0:T(8,128)(2,1)})) %all-reduce.6.cloned.1.call-update) | async-done | bytes 2162704 | tf_op jit(solution)/shard_map/psum | solution.py:196
  331.3 1.8 convert_element_type.82
  333.2 2.0 slice.195
  336.6 1.1 convert_element_type.84
  (134 shorter events, 16.1 us)
Async XLA Ops:
  7.2 6.6 %copy-start = (f32[16,49]{1,0:T(8,128)S(1)}, f32[16,49]{1,0:T(8,128)}, u32[]{:S(2)}) copy-start(f32[16,49]{1,0:T(8,128)} %param.20) | copy-start | bytes 9412
  7.2 172.7 %reduce-scatter.5.cloned.1.call-start = ((), (), s32[]{:S(2)}) async-start(), calls=%async_computation.3 | async-start | bytes 2621440 | tf_op jit(solution)/shard_map/reduce_scatter | solution.py:125
  7.2 38.6 %collective-permute-start = (bf16[256,3072]{1,0:T(8,128)(2,1)}, bf16[256,3072]{1,0:T(8,128)(2,1)}, u32[]{:S(2)}, u32[]{:S(2)}) collective-permute-start(bf16[256,3072]{1,0:T(8,128)(2,1)} %param.17), channel_id=1, source_target_pairs={{0,8},{4,12},{8,0},{12,4},{1,9},{5,13},{9,1},{13,5},{2,10},{6,14},... | collective-permute-start | bytes 4718600 | tf_op jit(solution)/shard_map/ppermute | solution.py:36
  10.3 50.5 %collective-permute-start.1 = (bf16[256,3072]{1,0:T(8,128)(2,1)}, bf16[256,3072]{1,0:T(8,128)(2,1)}, u32[]{:S(2)}, u32[]{:S(2)}) collective-permute-start(bf16[256,3072]{1,0:T(8,128)(2,1)} %param.17), channel_id=1, source_target_pairs={{0,4},{4,0},{8,12},{12,8},{1,5},{5,1},{9,13},{13,9},{2,6},{6,2},{1... | collective-permute-start | bytes 4718600 | tf_op jit(solution)/shard_map/ppermute | solution.py:39
  10.3 47.2 %collective-permute-start.7 = (bf16[256,1024]{1,0:T(8,128)(2,1)}, bf16[256,1024]{1,0:T(8,128)(2,1)}, u32[]{:S(2)}, u32[]{:S(2)}) collective-permute-start(bf16[256,1024]{1,0:T(8,128)(2,1)} %param.18), channel_id=1, source_target_pairs={{0,8},{4,12},{8,0},{12,4},{1,9},{5,13},{9,1},{13,5},{2,10},{6,14},... | collective-permute-start | bytes 1572872 | tf_op jit(solution)/shard_map/ppermute | solution.py:36
  10.4 59.6 %collective-permute-start.8 = (bf16[256,1024]{1,0:T(8,128)(2,1)}, bf16[256,1024]{1,0:T(8,128)(2,1)}, u32[]{:S(2)}, u32[]{:S(2)}) collective-permute-start(bf16[256,1024]{1,0:T(8,128)(2,1)} %param.18), channel_id=1, source_target_pairs={{0,4},{4,0},{8,12},{12,8},{1,5},{5,1},{9,13},{13,9},{2,6},{6,2},{1... | collective-permute-start | bytes 1572872 | tf_op jit(solution)/shard_map/ppermute | solution.py:39
  13.2 32.6 %copy-start.10 = (bf16[8,16,1024]{2,1,0:T(8,128)(2,1)S(1)}, bf16[8,16,1024]{2,1,0:T(8,128)(2,1)}, u32[]{:S(2)}) copy-start(bf16[8,16,1024]{2,1,0:T(8,128)(2,1)} %param.15) | copy-start | bytes 786436
  13.2 32.6 %copy-start.29 = (f32[1024]{0:T(1024)S(1)}, f32[1024]{0:T(1024)}, u32[]{:S(2)}) copy-start(f32[1024]{0:T(1024)} %param.19) | copy-start | bytes 12292
  13.8 32.0 %copy-start.18 = (s32[43008]{0:T(1024)}, s32[43008]{0:T(1024)S(1)}, u32[]{:S(2)}) copy-start(s32[43008]{0:T(1024)S(1)} %reshape.409) | copy-start | bytes 516100
  13.8 32.3 %copy-start.34 = (s32[8,16]{1,0:T(8,128)S(1)}, s32[8,16]{1,0:T(8,128)}, u32[]{:S(2)}) copy-start(s32[8,16]{1,0:T(8,128)} %param.21) | copy-start | bytes 1540
  45.8 16.5 %collective-permute-start.2 = (bf16[256,3072]{1,0:T(8,128)(2,1)}, bf16[256,3072]{1,0:T(8,128)(2,1)}, u32[]{:S(2)}, u32[]{:S(2)}) collective-permute-start(bf16[256,3072]{1,0:T(8,128)(2,1)} %collective-permute-done), channel_id=1, source_target_pairs={{0,4},{4,0},{8,12},{12,8},{1,5},{5,1},{9,13},{13,9},{2,6},{6,2},{1... | collective-permute-start | bytes 4718600 | tf_op jit(solution)/shard_map/ppermute | solution.py:39
  46.1 17.9 %copy-start.8 = (bf16[8,16,1024]{2,1,0:T(8,128)(2,1)}, bf16[8,16,1024]{2,1,0:T(8,128)(2,1)S(1)}, u32[]{:S(2)}) copy-start(bf16[8,16,1024]{2,1,0:T(8,128)(2,1)S(1)} %fusion.50) | copy-start | bytes 786436
  53.1 2.7 copy-start.26
  55.9 1.4 copy-start.17
  57.5 13.6 %collective-permute-start.9 = (bf16[256,1024]{1,0:T(8,128)(2,1)}, bf16[256,1024]{1,0:T(8,128)(2,1)S(1)}, u32[]{:S(2)}, u32[]{:S(2)}) collective-permute-start(bf16[256,1024]{1,0:T(8,128)(2,1)} %collective-permute-done.7), channel_id=1, source_target_pairs={{0,4},{4,0},{8,12},{12,8},{1,5},{5,1},{9,13},{13,9},{2,6},{6,2},{1... | collective-permute-start | bytes 1572872 | tf_op jit(solution)/shard_map/ppermute | solution.py:39
  63.9 2.6 copy-start.2
  64.0 2.7 copy-start.33
  66.6 13.8 %copy-start.13 = (bf16[8,16,1024]{2,1,0:T(8,128)(2,1)S(1)}, bf16[8,16,1024]{2,1,0:T(8,128)(2,1)}, u32[]{:S(2)}) copy-start(bf16[8,16,1024]{2,1,0:T(8,128)(2,1)} %param.16) | copy-start | bytes 786436
  66.7 15.1 %copy-start.25 = (bf16[8,16,128]{2,1,0:T(8,128)(2,1)}, bf16[8,16,128]{2,1,0:T(8,128)(2,1)S(1)}, u32[]{:S(2)}) copy-start(bf16[8,16,128]{2,1,0:T(8,128)(2,1)S(1)} %broadcast_in_dim.46) | copy-start | bytes 98308
  66.8 4.4 %collective-permute-start.3 = (bf16[3,16,2176]{2,1,0:T(8,128)(2,1)S(1)}, bf16[3,16,2176]{2,1,0:T(8,128)(2,1)S(1)}, u32[]{:S(2)}, u32[]{:S(2)}) collective-permute-start(bf16[3,16,2176]{2,1,0:T(8,128)(2,1)S(1)} %get-tuple-element.66), channel_id=1, source_target_pairs={{0,4},{4,8},{8,12},{1,5},{5,9},{9,13},{2,6},{6,10},{10,14},{3,7},{... | collective-permute-start | bytes 626696 | tf_op jit(solution)/shard_map/ppermute | solution.py:18
  68.7 5.0 %collective-permute-start.4 = (bf16[3,16,2176]{2,1,0:T(8,128)(2,1)S(1)}, bf16[3,16,2176]{2,1,0:T(8,128)(2,1)S(1)}, u32[]{:S(2)}, u32[]{:S(2)}) collective-permute-start(bf16[3,16,2176]{2,1,0:T(8,128)(2,1)S(1)} %get-tuple-element.67), channel_id=1, source_target_pairs={{4,0},{8,4},{12,8},{5,1},{9,5},{13,9},{6,2},{10,6},{14,10},{7,3},{... | collective-permute-start | bytes 626696 | tf_op jit(solution)/shard_map/ppermute | solution.py:19
  71.2 10.6 %copy-start.21 = (bf16[3,16,2176]{2,1,0:T(8,128)(2,1)}, bf16[3,16,2176]{2,1,0:T(8,128)(2,1)S(1)}, u32[]{:S(2)}) copy-start(bf16[3,16,2176]{2,1,0:T(8,128)(2,1)S(1)} %collective-permute-done.3) | copy-start | bytes 626692
  73.7 8.1 %copy-start.22 = (bf16[3,16,2176]{2,1,0:T(8,128)(2,1)}, bf16[3,16,2176]{2,1,0:T(8,128)(2,1)S(1)}, u32[]{:S(2)}) copy-start(bf16[3,16,2176]{2,1,0:T(8,128)(2,1)S(1)} %collective-permute-done.4) | copy-start | bytes 626692
  74.7 8.0 %collective-permute-start.5 = (bf16[14,3,2176]{2,1,0:T(4,128)(2,1)}, bf16[14,3,2176]{2,1,0:T(4,128)(2,1)}, u32[]{:S(2)}, u32[]{:S(2)}) collective-permute-start(bf16[14,3,2176]{2,1,0:T(4,128)(2,1)} %get-tuple-element.62), channel_id=1, source_target_pairs={{0,1},{1,2},{2,3},{4,5},{5,6},{6,7},{8,9},{9,10},{10,11},{12,13},{... | collective-permute-start | bytes 548360 | tf_op jit(solution)/shard_map/ppermute | solution.py:18
  78.9 8.4 %collective-permute-start.6 = (bf16[14,3,2176]{2,1,0:T(4,128)(2,1)}, bf16[14,3,2176]{2,1,0:T(4,128)(2,1)}, u32[]{:S(2)}, u32[]{:S(2)}) collective-permute-start(bf16[14,3,2176]{2,1,0:T(4,128)(2,1)} %get-tuple-element.63), channel_id=1, source_target_pairs={{1,0},{2,1},{3,2},{5,4},{6,5},{7,6},{9,8},{10,9},{11,10},{13,12},{... | collective-permute-start | bytes 548360 | tf_op jit(solution)/shard_map/ppermute | solution.py:19
  90.3 5.7 %copy-start.31 = (s32[336]{0:T(512)S(1)}, s32[336]{0:T(512)}, u32[]{:S(2)}) copy-start(s32[336]{0:T(512)} %iota.108) | copy-start | bytes 4036
  90.3 5.6 %copy-start.32 = (s32[336]{0:T(512)S(1)}, s32[336]{0:T(512)}, u32[]{:S(2)}) copy-start(s32[336]{0:T(512)} %iota.114) | copy-start | bytes 4036
  98.7 1.1 copy-start.23
  98.7 1.2 copy-start.27
  120.4 1.8 copy-start.7
  122.2 8.4 %copy-start.14 = (bf16[8,16,1024]{2,1,0:T(8,128)(2,1)S(1)}, bf16[8,16,1024]{2,1,0:T(8,128)(2,1)}, u32[]{:S(2)}) copy-start(bf16[8,16,1024]{2,1,0:T(8,128)(2,1)} %param.16) | copy-start | bytes 786436
  122.2 8.4 %copy-start.28 = (bf16[16,64,128]{2,1,0:T(8,128)(2,1)S(1)}, bf16[16,64,128]{2,1,0:T(8,128)(2,1)}, u32[]{:S(2)}) copy-start(bf16[16,64,128]{2,1,0:T(8,128)(2,1)} %get-tuple-element.71) | copy-start | bytes 786436
  122.3 1.6 copy-start.5
  125.0 20.8 %collective-permute-start.10 = (f32[3,22,2048]{2,1,0:T(8,128)}, f32[3,22,2048]{2,1,0:T(8,128)}, u32[]{:S(2)}, u32[]{:S(2)}) collective-permute-start(f32[3,22,2048]{2,1,0:T(8,128)} %get-tuple-element.59), channel_id=1, source_target_pairs={{0,4},{4,8},{8,12},{1,5},{5,9},{9,13},{2,6},{6,10},{10,14},{3,7},{... | collective-permute-start | bytes 1622024 | tf_op jit(solution)/shard_map/ppermute | solution.py:27
  132.7 106.6 %reduce-scatter.3.cloned.1.call-start = ((), (), s32[]{:S(2)}) async-start(), calls=%async_computation.2 | async-start | bytes 8192000 | tf_op jit(solution)/shard_map/reduce_scatter | solution.py:196
  132.7 3.7 %copy-start.6 = (f32[14,24,2048]{2,1,0:T(8,128)S(1)}, f32[14,24,2048]{2,1,0:T(8,128)}, u32[]{:S(2)}) copy-start(f32[14,24,2048]{2,1,0:T(8,128)} %copy-done.5) | copy-start | bytes 8257540
  133.3 13.8 %collective-permute-start.11 = (f32[3,22,2048]{2,1,0:T(8,128)}, f32[3,22,2048]{2,1,0:T(8,128)}, u32[]{:S(2)}, u32[]{:S(2)}) collective-permute-start(f32[3,22,2048]{2,1,0:T(8,128)} %get-tuple-element.58), channel_id=1, source_target_pairs={{4,0},{8,4},{12,8},{5,1},{9,5},{13,9},{6,2},{10,6},{14,10},{7,3},{... | collective-permute-start | bytes 1622024 | tf_op jit(solution)/shard_map/ppermute | solution.py:27
  140.0 5.7 %copy-start.3 = (f32[8,22,2048]{2,1,0:T(8,128)S(1)}, f32[8,22,2048]{2,1,0:T(8,128)}, u32[]{:S(2)}) copy-start(f32[8,22,2048]{2,1,0:T(8,128)} %slice.185) | copy-start | bytes 4325380
  147.1 5.1 %copy-start.12 = (f32[4,4,43008]{2,1,0:T(4,128)S(1)}, f32[4,4,43008]{2,1,0:T(4,128)}, u32[]{:S(2)}) copy-start(f32[4,4,43008]{2,1,0:T(4,128)} %dot_general.55) | copy-start | bytes 8257540
  147.1 5.1 %copy-start.19 = (s32[43008]{0:T(1024)S(1)}, s32[43008]{0:T(1024)}, u32[]{:S(2)}) copy-start(s32[43008]{0:T(1024)} %copy-done.18) | copy-start | bytes 516100
  148.5 7.5 %copy-start.16 = (bf16[16,64,128]{2,1,0:T(8,128)(2,1)S(1)}, bf16[16,64,128]{2,1,0:T(8,128)(2,1)}, u32[]{:S(2)}) copy-start(bf16[16,64,128]{2,1,0:T(8,128)(2,1)} %fusion.22) | copy-start | bytes 786436
  149.4 10.4 %collective-permute-start.12 = (bf16[8,3,2048]{2,1,0:T(4,128)(2,1)S(1)}, bf16[8,3,2048]{2,1,0:T(4,128)(2,1)S(1)}, u32[]{:S(2)}, u32[]{:S(2)}) collective-permute-start(bf16[8,3,2048]{2,1,0:T(4,128)(2,1)S(1)} %get-tuple-element.65), channel_id=1, source_target_pairs={{0,1},{1,2},{2,3},{4,5},{5,6},{6,7},{8,9},{9,10},{10,11},{12,13},{... | collective-permute-start | bytes 294920 | tf_op jit(solution)/shard_map/ppermute | solution.py:27
  158.3 10.3 %copy-start.11 = (bf16[8,16,1024]{2,1,0:T(8,128)(2,1)S(1)}, bf16[8,16,1024]{2,1,0:T(8,128)(2,1)}, u32[]{:S(2)}) copy-start(bf16[8,16,1024]{2,1,0:T(8,128)(2,1)} %param.15) | copy-start | bytes 786436
  158.3 10.3 %copy-start.30 = (f32[1024]{0:T(1024)S(1)}, f32[1024]{0:T(1024)}, u32[]{:S(2)}) copy-start(f32[1024]{0:T(1024)} %param.19) | copy-start | bytes 12292
  158.5 8.4 %collective-permute-start.13 = (bf16[8,3,2048]{2,1,0:T(4,128)(2,1)}, bf16[8,3,2048]{2,1,0:T(4,128)(2,1)}, u32[]{:S(2)}, u32[]{:S(2)}) collective-permute-start(bf16[8,3,2048]{2,1,0:T(4,128)(2,1)} %get-tuple-element.64), channel_id=1, source_target_pairs={{1,0},{2,1},{3,2},{5,4},{6,5},{7,6},{9,8},{10,9},{11,10},{13,12},{... | collective-permute-start | bytes 294920 | tf_op jit(solution)/shard_map/ppermute | solution.py:27
  168.7 5.5 %copy-start.9 = (bf16[8,16,1024]{2,1,0:T(8,128)(2,1)S(1)}, bf16[8,16,1024]{2,1,0:T(8,128)(2,1)}, u32[]{:S(2)}) copy-start(bf16[8,16,1024]{2,1,0:T(8,128)(2,1)} %copy-done.8) | copy-start | bytes 786436
  174.2 4.7 %copy-start.20 = (bf16[4,256,49]{2,1,0:T(8,128)(2,1)S(1)}, bf16[4,256,49]{2,1,0:T(8,128)(2,1)}, u32[]{:S(2)}) copy-start(bf16[4,256,49]{2,1,0:T(8,128)(2,1)} %pad.23) | copy-start | bytes 301060
  174.2 4.7 %copy-start.35 = (bf16[128]{0:T(256)(128)(2,1)S(1)}, bf16[128]{0:T(256)(128)(2,1)}, u32[]{:S(2)}) copy-start(bf16[128]{0:T(256)(128)(2,1)} %pad.26.clone) | copy-start | bytes 772
  179.8 59.5 %copy-start.15 = (bf16[8,16,1024]{2,1,0:T(8,128)(2,1)S(1)}, bf16[8,16,1024]{2,1,0:T(8,128)(2,1)}, u32[]{:S(2)}) copy-start(bf16[8,16,1024]{2,1,0:T(8,128)(2,1)} %param.16) | copy-start | bytes 786436
  179.8 151.5 %all-reduce.6.cloned.1.call-start = ((), (), s32[]{:S(2)}) async-start(), calls=%async_computation.4 | async-start | bytes 4325376 | tf_op jit(solution)/shard_map/psum | solution.py:196
  331.3 1.9 copy-start.4
  331.3 6.4 %copy-start.1 = (f32[16,49]{1,0:T(8,128)S(1)}, f32[16,49]{1,0:T(8,128)}, u32[]{:S(2)}) copy-start(f32[16,49]{1,0:T(8,128)} %param.20) | copy-start | bytes 9412
  333.2 3.4 copy-start.24
Sparse Core Ops, SparseCore 0:
  132.8 30.0 reduce-scatter.4
  179.9 59.2 reduce-scatter.2
  241.7 89.5 all-reduce.5
